TPU v7x, 256 devices: a whole 4x4x8 slice. The times are simulated.
256 devices in a mesh: expert: 32 (over z, x), helper: 8 (over y, core).
Axes of the slice: x: 4, y: 4, z: 8, core: 2. Of those that a mesh axis runs over, the one named last changes fastest.
Arguments:
- route_ids: int32 [65536], P(('expert', 'helper')), may hold values from 0 to 255, as said below
- hot_expert: int32 [256], replicated, may hold values from 0 to 255, as said below
- features: bfloat16 [65536, 1024], P(('expert', 'helper')), may hold values from -6 to 6
- tangents: bfloat16 [3, 65536, 1024], P(None, ('expert', 'helper')), may hold values from -6 to 6
- expert_weight: bfloat16 [256, 1024, 1024], P(('expert', 'helper')), may hold values from -0.1875 to 0.1875
- expert_bias: bfloat16 [256, 1024], P(('expert', 'helper')), may hold values from -3 to 3
- cot_value: bfloat16 [65536, 1024], P(('expert', 'helper')), may hold values from -0.375 to 0.375
- cot_tangent: bfloat16 [3, 65536, 1024], P(None, ('expert', 'helper')), may hold values from -0.375 to 0.375
Outputs:
- value_out: bfloat16 [65536, 1024], P(('expert', 'helper'))
- tangent_out: bfloat16 [3, 65536, 1024], P(None, ('expert', 'helper'))
- grad_weight: bfloat16 [256, 1024, 1024], P(('expert', 'helper'))
- grad_bias: float32 [256, 1024], P(('expert', 'helper'))
Inputs may be any that keep to these rules, and one draw needn't show every extreme that they name: `route_ids`: among the 256 points of each device, the expert hot_expert[0] is named 3 times; a quarter of the experts less one are named 2 times each, half of the experts less one are named once each, the rest never. `hot_expert`: each expert appears once; the first entry is the expert that every device names 3 times.
All inputs are finite; a program needn't handle non-finite values.
Results may differ from a plain program's by a relative error of at most 0.0049.
Values may be sent and summed in bfloat16 or wider, within the bound.
No kernel may reach another device: no remote copies, remote signals or barrier semaphores. Data moves between devices by JAX's collectives and lax.ppermute only.
A program may use at most 192 MiB of HBM per device.

v0:
```python
import jax
import jax.numpy as jnp
from jax import lax
from jax.sharding import PartitionSpec as P


def lower_ones(samples):
    index = jnp.arange(samples, dtype=jnp.int32)
    return (index[:, None] > index[None, :]).astype(jnp.bfloat16)


def slot_tables(route_ids, groups, capacity, triangle):
    samples = route_ids.shape[0]
    onehot = (route_ids[:, None] == jnp.arange(groups, dtype=jnp.int32)[None, :]).astype(
        jnp.bfloat16
    )
    before = jnp.dot(triangle, onehot, preferred_element_type=jnp.float32)
    rank_in = jnp.sum(before * onehot.astype(jnp.float32), axis=1).astype(jnp.int32)
    slot_of = route_ids * capacity + rank_in
    source = (
        jnp.full((groups * capacity,), samples, jnp.int32)
        .at[slot_of]
        .set(jnp.arange(samples, dtype=jnp.int32), mode="drop")
    )
    return (slot_of, source)


def forward_pass(inputs, weight, bias_row):
    slot_count = inputs.shape[1]
    feature_dim = inputs.shape[2]
    product = jnp.dot(
        inputs.reshape(4 * slot_count, feature_dim), weight, preferred_element_type=jnp.float32
    ).reshape(4, slot_count, feature_dim)
    preact = product[0] + bias_row[None, :]
    directed = product[1:]
    slopes = jax.nn.sigmoid(preact)
    values = jax.nn.softplus(preact).astype(jnp.bfloat16)
    carried = (slopes[None] * directed).astype(jnp.bfloat16)
    return (jnp.concatenate([values[None], carried], axis=0), slopes, directed)


def backward_pass(inputs, slopes, directed, cotangent):
    slot_count = inputs.shape[1]
    feature_dim = inputs.shape[2]
    cot_float = cotangent.astype(jnp.float32)
    grad_pre = cot_float[0] * slopes + jnp.sum(cot_float[1:] * directed, axis=0) * slopes * (
        1.0 - slopes
    )
    grad_dir = (cot_float[1:] * slopes[None]).astype(jnp.bfloat16)
    gradients = jnp.concatenate([grad_pre.astype(jnp.bfloat16)[None], grad_dir], axis=0).reshape(
        4 * slot_count, feature_dim
    )
    weight_grad = lax.dot_general(
        inputs.reshape(4 * slot_count, feature_dim),
        gradients,
        (((0,), (0,)), ((), ())),
        preferred_element_type=jnp.float32,
    )
    return (weight_grad, jnp.sum(grad_pre, axis=0))


def send_back(results, slot_of, n_expert, n_helper, capacity):
    stack_depth = results.shape[0]
    feature_dim = results.shape[2]
    returned = lax.all_to_all(
        lax.all_to_all(
            results.reshape(stack_depth, n_expert, n_helper, capacity, feature_dim),
            "expert",
            split_axis=1,
            concat_axis=1,
            tiled=True,
        ),
        "helper",
        split_axis=2,
        concat_axis=2,
        tiled=True,
    )
    return jnp.take(
        returned.reshape(stack_depth, n_expert * n_helper * capacity, feature_dim),
        slot_of,
        axis=1,
        mode="fill",
        fill_value=0,
    )


def body(
    route_ids, hot_expert, features, tangents, expert_weight, expert_bias, cot_value, cot_tangent
):
    n_expert = lax.axis_size("expert")
    n_helper = lax.axis_size("helper")
    groups = n_expert * n_helper
    samples = route_ids.shape[0]
    feature_dim = features.shape[1]
    cap_small = 2 * samples // groups
    hot_count = 3 * cap_small // 2
    triangle = lower_ones(samples)
    slot_count = groups * hot_count
    slot_of, source = slot_tables(route_ids, groups, hot_count, triangle)

    def arrange(stacked):
        stack_depth = stacked.shape[0]
        placed = jnp.take(stacked, source, axis=1, mode="fill", fill_value=0)
        return placed.reshape(stack_depth, n_expert, n_helper, hot_count, feature_dim)

    inputs_local = jnp.concatenate([features[None], tangents], axis=0)
    cot_local = jnp.concatenate([cot_value[None], cot_tangent], axis=0)
    inputs = lax.all_to_all(
        lax.all_to_all(arrange(inputs_local), "expert", split_axis=1, concat_axis=1, tiled=True),
        "helper",
        split_axis=2,
        concat_axis=2,
        tiled=True,
    )
    inputs = inputs.reshape(4, slot_count, feature_dim)
    results, slopes, directed = forward_pass(inputs, expert_weight[0], expert_bias[0])
    returned = send_back(results, slot_of, n_expert, n_helper, hot_count)
    cotangent = lax.all_to_all(
        lax.all_to_all(arrange(cot_local), "expert", split_axis=1, concat_axis=1, tiled=True),
        "helper",
        split_axis=2,
        concat_axis=2,
        tiled=True,
    )
    cotangent = cotangent.reshape(4, slot_count, feature_dim)
    weight_grad, bias_grad = backward_pass(inputs, slopes, directed, cotangent)
    return (returned[0], returned[1:], weight_grad.astype(jnp.bfloat16)[None], bias_grad[None])


def solution(mesh):
    return jax.shard_map(
        body,
        mesh=mesh,
        in_specs=(
            P(("expert", "helper")),
            P(),
            P(("expert", "helper"), None),
            P(None, ("expert", "helper"), None),
            P(("expert", "helper"), None, None),
            P(("expert", "helper"), None),
            P(("expert", "helper"), None),
            P(None, ("expert", "helper"), None),
        ),
        out_specs=(
            P(("expert", "helper"), None),
            P(None, ("expert", "helper"), None),
            P(("expert", "helper"), None, None),
            P(("expert", "helper"), None),
        ),
        check_vma=False,
    )
```

profile of v0, /device:TPU:1, one launch (start us, length us, event | category | flops | bytes accessed | tf_op | source)
XLA Modules:
  0.0 928.8 jit_solution(14993953677911027597)
XLA Ops:
  17.6 23.9 %gather_fusion.2 = bf16[768,4,1024]{2,1,0:T(4,128)(2,1)} fusion(bf16[4,256,1024]{2,0,1:T(4,128)(2,1)} %pad_maximum_fusion.3, s32[1024]{0:T(1024)S(1)} %pad_clamp_fusion.1), kind=kCustom, calls=%fused_computation.1.clone | custom fusion | bytes 12585984 | tf_op jit(solution)/shard_map/jit(_take)/gather | solution.py:103
  41.5 24.3 %gather_fusion.1 = bf16[768,4,1024]{2,1,0:T(4,128)(2,1)} fusion(bf16[4,256,1024]{2,0,1:T(4,128)(2,1)} %pad_maximum_fusion.2, s32[1024]{0:T(1024)S(1)} %pad_clamp_fusion.1), kind=kCustom, calls=%fused_computation.clone | custom fusion | bytes 12585984 | tf_op jit(solution)/shard_map/jit(_take)/gather | solution.py:103
  65.7 11.4 %broadcast_select_fusion = (bf16[768,4,1024]{2,1,0:T(4,128)(2,1)}, bf16[768,4,1024]{2,1,0:T(4,128)(2,1)S(1)}) fusion(bf16[768,4,1024]{2,1,0:T(4,128)(2,1)} %gather_fusion.2, pred[768]{0:T(1024)(128)(4,1)S(1)} %compare_and_fusion, bf16[768,4,1024]{2,1,0:T(4,128)(2,1)} %gather_fusion.1), kind=kLoop, calls=%fused_computation.10 | loop fusion | flops 6291456 | bytes 25166592 | tf_op jit(solution)/shard_map/jit(_take)/select_n | solution.py:103
  77.1 150.2 %all_to_all.30 = bf16[4,32,8,3,1024]{4,0,3,2,1:T(4,128)(2,1)} all-to-all(bf16[4,32,8,3,1024]{4,0,3,2,1:T(4,128)(2,1)S(1)} %bitcast.38), channel_id=1, replica_groups=mesh['expert'=32,'helper'=8] {'expert'}, dimensions={1} | all-to-all | bytes 12582912 | tf_op jit(solution)/shard_map/all_to_all | solution.py:109
  227.4 6.5 all-to-all-start.4
  233.9 8.1 copy.29
  241.9 127.9 %all-to-all-done.4 = bf16[4,32,8,3,1024]{4,0,3,2,1:T(4,128)(2,1)} async-done(((bf16[4,32,8,3,1024]{4,0,3,2,1:T(4,128)(2,1)}), bf16[4,32,8,3,1024]{4,0,3,2,1:T(4,128)(2,1)}, u32[]{:S(2)}, u32[]{:S(2)}) %all-to-all-start.4) | async-done | bytes 6291488 | tf_op jit(solution)/shard_map/all_to_all | solution.py:119
  369.8 10.4 %all-to-all-start.1 = ((bf16[4,32,8,3,1024]{4,0,3,1,2:T(4,128)(2,1)}), bf16[4,32,8,3,1024]{4,0,3,1,2:T(4,128)(2,1)}, u32[]{:S(2)}, u32[]{:S(2)}) async-start(bf16[4,32,8,3,1024]{4,0,3,1,2:T(4,128)(2,1)} %copy.29), calls=%async_computation.1 | async-start | bytes 12582912 | tf_op jit(solution)/shard_map/all_to_all | solution.py:108
  380.2 8.0 copy.36
  388.2 63.3 %all-to-all-done.1 = bf16[4,32,8,3,1024]{4,0,3,1,2:T(4,128)(2,1)} async-done(((bf16[4,32,8,3,1024]{4,0,3,1,2:T(4,128)(2,1)}), bf16[4,32,8,3,1024]{4,0,3,1,2:T(4,128)(2,1)}, u32[]{:S(2)}, u32[]{:S(2)}) %all-to-all-start.1) | async-done | bytes 6291488 | tf_op jit(solution)/shard_map/all_to_all | solution.py:108
  451.5 5.9 all-to-all-start.5
  457.4 10.9 %copy.30 = bf16[4,32,8,3,1024]{4,3,2,1,0:T(4,128)(2,1)} copy(bf16[4,32,8,3,1024]{4,0,3,1,2:T(4,128)(2,1)} %all-to-all-done.1) | data formatting | bytes 12582912 | tf_op jit(solution)/shard_map/all_to_all | solution.py:108
  468.3 16.3 %reshape_reshape.4 = bf16[3072,1024]{1,0:T(8,128)(2,1)} reshape(bf16[4,32,8,3,1024]{4,3,2,1,0:T(4,128)(2,1)} %copy.30) | data formatting | bytes 12582912 | tf_op jit(solution)/shard_map/reshape;reshape | solution.py:32
  484.6 44.0 %all-to-all-done.5 = bf16[4,32,8,3,1024]{4,0,3,1,2:T(4,128)(2,1)} async-done(((bf16[4,32,8,3,1024]{4,0,3,1,2:T(4,128)(2,1)}), bf16[4,32,8,3,1024]{4,0,3,1,2:T(4,128)(2,1)}, u32[]{:S(2)}, u32[]{:S(2)}) %all-to-all-start.5) | async-done | bytes 6291488 | tf_op jit(solution)/shard_map/all_to_all | solution.py:118
  537.8 5.9 squeeze.15
  543.7 11.3 %slice.52 = f32[3,32,8,3,1024]{4,0,3,1,2:T(4,128)} slice(bf16[4,32,8,3,1024]{4,0,3,1,2:T(4,128)(2,1)} %all-to-all-done.5), slice={[1:4], [0:32], [0:8], [0:3], [0:1024]} | slice | bytes 18874368 | tf_op jit(solution)/shard_map/slice | solution.py:46
  555.1 15.8 %copy.39 = f32[3,32,8,3,1024]{4,3,2,1,0:T(4,128)} copy(f32[3,32,8,3,1024]{4,0,3,1,2:T(4,128)} %slice.52) | data formatting | bytes 18874368 | tf_op jit(solution)/shard_map/slice | solution.py:46
  570.9 15.0 %slice.39 = f32[3,768,1024]{2,1,0:T(8,128)} reshape(f32[3,32,8,3,1024]{4,3,2,1,0:T(4,128)} %copy.39) | data formatting | bytes 18874368 | tf_op jit(solution)/shard_map/slice | solution.py:46
  585.9 9.0 fusion.2
  604.0 14.5 %slice.33 = f32[3,32,8,3,1024]{4,3,2,1,0:T(4,128)} reshape(f32[2304,1024]{1,0:T(8,128)} %slice.48) | data formatting | bytes 18874368 | tf_op jit(solution)/shard_map/slice | solution.py:35
  618.6 10.7 %multiply_reduce_fusion = f32[768,1024]{1,0:T(8,128)} fusion(f32[3,768,1024]{2,1,0:T(8,128)} %slice.39, f32[3,768,1024]{2,1,0:T(8,128)} %bitcast.36), kind=kLoop, calls=%fused_computation.7 | loop fusion | flops 3932160 | bytes 22020096 | tf_op jit(solution)/shard_map/reduce_sum | solution.py:46
  629.2 9.0 add_reduce_fusion
  644.0 6.9 fusion
  656.7 8.7 multiply_convert_fusion
  671.0 6.7 copy.31
  677.7 144.1 %all_to_all.31 = bf16[4,32,8,3,1024]{4,2,3,0,1:T(8,128)(2,1)S(1)} all-to-all(bf16[4,32,8,3,1024]{4,2,3,0,1:T(8,128)(2,1)} %copy.31), channel_id=1, replica_groups=mesh['expert'=32,'helper'=8] {'expert'}, dimensions={1} | all-to-all | bytes 12582912 | tf_op jit(solution)/shard_map/all_to_all | solution.py:66
  821.8 6.2 copy.32
  828.0 7.6 all-to-all-start.3
  842.9 7.7 multiply_convert_fusion.1
  853.5 10.0 %convert_bitcast_fusion = bf16[1,1024,1024]{2,1,0:T(8,128)(2,1)} fusion(bf16[3072,1024]{1,0:T(8,128)(2,1)} %reshape_reshape.4, bf16[3072,1024]{1,0:T(8,128)(2,1)S(1)} %bitcast.41), kind=kOutput, calls=%fused_computation.24 | convolution fusion | flops 6443499520 | bytes 14680064 | tf_op jit(solution)/shard_map/dot_general | solution.py:53
  863.5 43.4 %all-to-all-done.3 = bf16[4,32,8,3,1024]{4,1,3,0,2:T(8,128)(2,1)} async-done(((bf16[4,32,8,3,1024]{4,1,3,0,2:T(8,128)(2,1)}), bf16[4,32,8,3,1024]{4,1,3,0,2:T(8,128)(2,1)}, u32[]{:S(2)}, u32[]{:S(2)}) %all-to-all-start.3) | async-done | bytes 6291488 | tf_op jit(solution)/shard_map/all_to_all | solution.py:65
  906.9 10.3 %copy.33 = bf16[4,32,8,3,1024]{4,0,3,2,1:T(4,128)(2,1)} copy(bf16[4,32,8,3,1024]{4,1,3,0,2:T(8,128)(2,1)} %all-to-all-done.3) | data formatting | bytes 12582912 | tf_op jit(solution)/shard_map/all_to_all | solution.py:65
  (50 shorter events, 73.8 us)
Async XLA Ops:
  0.6 585.2 %copy-start = (bf16[1,1024,1024]{2,1,0:T(8,128)(2,1)S(1)}, bf16[1,1024,1024]{2,1,0:T(8,128)(2,1)}, u32[]{:S(2)}) copy-start(bf16[1,1024,1024]{2,1,0:T(8,128)(2,1)} %param.13) | copy-start | bytes 6291460
  4.4 3.9 copy-start.6
  4.4 5.3 copy-start.7
  227.4 142.5 %all-to-all-start.4 = ((bf16[4,32,8,3,1024]{4,0,3,2,1:T(4,128)(2,1)}), bf16[4,32,8,3,1024]{4,0,3,2,1:T(4,128)(2,1)}, u32[]{:S(2)}, u32[]{:S(2)}) async-start(bf16[4,32,8,3,1024]{4,0,3,2,1:T(4,128)(2,1)} %bitcast.37), calls=%async_computation.4 | async-start | bytes 12582912 | tf_op jit(solution)/shard_map/all_to_all | solution.py:119
  369.8 81.6 %all-to-all-start.1 = ((bf16[4,32,8,3,1024]{4,0,3,1,2:T(4,128)(2,1)}), bf16[4,32,8,3,1024]{4,0,3,1,2:T(4,128)(2,1)}, u32[]{:S(2)}, u32[]{:S(2)}) async-start(bf16[4,32,8,3,1024]{4,0,3,1,2:T(4,128)(2,1)} %copy.29), calls=%async_computation.1 | async-start | bytes 12582912 | tf_op jit(solution)/shard_map/all_to_all | solution.py:108
  388.2 69.1 %copy-start.8 = (bf16[1,1024]{1,0:T(2,128)(2,1)S(1)}, bf16[1,1024]{1,0:T(2,128)(2,1)}, u32[]{:S(2)}) copy-start(bf16[1,1024]{1,0:T(2,128)(2,1)} %param.14) | copy-start | bytes 6148
  451.5 77.1 %all-to-all-start.5 = ((bf16[4,32,8,3,1024]{4,0,3,1,2:T(4,128)(2,1)}), bf16[4,32,8,3,1024]{4,0,3,1,2:T(4,128)(2,1)}, u32[]{:S(2)}, u32[]{:S(2)}) async-start(bf16[4,32,8,3,1024]{4,0,3,1,2:T(4,128)(2,1)} %copy.36), calls=%async_computation.5 | async-start | bytes 12582912 | tf_op jit(solution)/shard_map/all_to_all | solution.py:118
  533.0 1.6 copy-start.3
  594.9 4.5 copy-start.5
  828.0 78.9 %all-to-all-start.3 = ((bf16[4,32,8,3,1024]{4,1,3,0,2:T(8,128)(2,1)}), bf16[4,32,8,3,1024]{4,1,3,0,2:T(8,128)(2,1)}, u32[]{:S(2)}, u32[]{:S(2)}) async-start(bf16[4,32,8,3,1024]{4,1,3,0,2:T(8,128)(2,1)} %copy.32), calls=%async_computation.3 | async-start | bytes 12582912 | tf_op jit(solution)/shard_map/all_to_all | solution.py:65
  835.6 5.6 copy-start.2
  835.6 5.6 copy-start.4
  917.2 5.3 copy-start.9
  923.9 4.6 copy-start.1
where the time goes:
time: 936 us; the launch traced here: 929 us
  blocking collectives  294 us (31%)
  waiting for transfers between devices  279 us (30%)
  local copies, waits for them, and re-layouts  231 us (25%)
  other arithmetic  73.6 us (8%)
  starting transfers between devices  30.3 us (3%)
  matrix products  20.1 us (2%)
    all_to_all x1, blocking collectives, body(): lax.all_to_all(arrange(inputs_local), 'expert', split_axis=1, concat_axis...  150 us
    all_to_all x1, blocking collectives, send_back(): lax.all_to_all(results.reshape(stack_depth, n_expert, n_helper, capacity,...  144 us
    all_to_all x1, waiting for transfers between devices, body(): lax.all_to_all(arrange(cot_local), 'expert', split_axis=1, concat_axis=1,...  128 us
    all_to_all x1, waiting for transfers between devices, body(): lax.all_to_all(lax.all_to_all(arrange(inputs_local), 'expert', split_axis...  63.3 us
    gather x2, local copies, waits for them, and re-layouts, arrange(): placed = jnp.take(stacked, source, axis=1, mode='fill', fill_value=0)  48.1 us
    all_to_all x1, waiting for transfers between devices, body(): lax.all_to_all(lax.all_to_all(arrange(cot_local), 'expert', split_axis=1,...  44 us
    all_to_all x1, waiting for transfers between devices, send_back(): lax.all_to_all(lax.all_to_all(results.reshape(stack_depth, n_expert, n_he...  43.4 us
    slice x3, local copies, waits for them, and re-layouts, backward_pass(): cot_float[1:] * directed  42.1 us
  transfers between devices with their start and end apart: 4, of which 4 were waited for; matrix products, arithmetic and copies ran while one was open for 8% of the time, Pallas kernels for 0%

commit v1 on v0

v1 whole, which is shorter than its diff:
```python
import jax
import jax.numpy as jnp
from jax import lax
from jax.sharding import PartitionSpec as P

AXES = ("expert", "helper")


def lower_ones(samples):
    index = jnp.arange(samples, dtype=jnp.int32)
    return (index[:, None] > index[None, :]).astype(jnp.bfloat16)


def ranks_of(route_ids, groups):
    samples = route_ids.shape[0]
    onehot = (route_ids[:, None] == jnp.arange(groups, dtype=jnp.int32)[None, :]).astype(
        jnp.bfloat16
    )
    before = jnp.dot(lower_ones(samples), onehot, preferred_element_type=jnp.float32)
    return jnp.sum(before * onehot.astype(jnp.float32), axis=1).astype(jnp.int32)


def expert_pass(inputs, cotangent, weight, bias_row):
    slot_count, depth, feature_dim = inputs.shape
    flat = inputs.reshape(slot_count * depth, feature_dim)
    product = jnp.dot(flat, weight, preferred_element_type=jnp.float32).reshape(
        slot_count, depth, feature_dim
    )
    preact = product[:, 0] + bias_row[None, :]
    directed = product[:, 1:]
    slopes = jax.nn.sigmoid(preact)
    values = jax.nn.softplus(preact).astype(jnp.bfloat16)
    carried = (slopes[:, None] * directed).astype(jnp.bfloat16)
    results = jnp.concatenate([values[:, None], carried], axis=1)
    cot_float = cotangent.astype(jnp.float32)
    grad_pre = cot_float[:, 0] * slopes + jnp.sum(cot_float[:, 1:] * directed, axis=1) * slopes * (
        1.0 - slopes
    )
    grad_dir = (cot_float[:, 1:] * slopes[:, None]).astype(jnp.bfloat16)
    gradients = jnp.concatenate([grad_pre.astype(jnp.bfloat16)[:, None], grad_dir], axis=1)
    weight_grad = lax.dot_general(
        flat,
        gradients.reshape(slot_count * depth, feature_dim),
        (((0,), (0,)), ((), ())),
        preferred_element_type=jnp.float32,
    )
    return results, weight_grad, jnp.sum(grad_pre, axis=0)


def body(
    route_ids, hot_expert, features, tangents, expert_weight, expert_bias, cot_value, cot_tangent
):
    n_expert = lax.axis_size("expert")
    n_helper = lax.axis_size("helper")
    groups = n_expert * n_helper
    samples = route_ids.shape[0]
    feature_dim = features.shape[1]
    cap = 2 * samples // groups
    me = lax.axis_index("expert") * n_helper + lax.axis_index("helper")
    is_hot = me == hot_expert[0]

    rank = ranks_of(route_ids, groups)
    slot = route_ids * cap + rank
    main = rank < cap
    dispatch = (
        (slot[None, :] == jnp.arange(groups * cap, dtype=jnp.int32)[:, None]) & main[None, :]
    ).astype(jnp.bfloat16)
    extra = jnp.logical_not(main)

    stacked = jnp.concatenate([features[None], tangents, cot_value[None], cot_tangent], axis=0)
    send = jnp.einsum(
        "sp,apd->sad", dispatch, stacked, preferred_element_type=jnp.float32
    ).astype(jnp.bfloat16)
    extra_rows = jnp.einsum(
        "p,apd->ad", extra.astype(jnp.bfloat16), stacked, preferred_element_type=jnp.float32
    ).astype(jnp.bfloat16)

    gathered = lax.all_gather(extra_rows, AXES, axis=0, tiled=False)
    gathered = jnp.where(is_hot, gathered, jnp.zeros_like(gathered))
    received = lax.all_to_all(
        send.reshape(groups, cap * 8, feature_dim), AXES, 0, 0, tiled=True
    ).reshape(groups * cap, 8, feature_dim)

    weight = expert_weight[0]
    bias_row = expert_bias[0]
    results, weight_grad, bias_grad = expert_pass(
        received[:, :4], received[:, 4:], weight, bias_row
    )
    extra_results, extra_wg, extra_bg = expert_pass(
        gathered[:, :4], gathered[:, 4:], weight, bias_row
    )

    returned = lax.all_to_all(
        results.reshape(groups, cap * 4, feature_dim), AXES, 0, 0, tiled=True
    ).reshape(groups * cap, 4, feature_dim)
    extra_results = jnp.where(is_hot, extra_results, jnp.zeros_like(extra_results))
    extra_back = lax.psum_scatter(extra_results, AXES, scatter_dimension=0, tiled=True)[0]

    combined = jnp.einsum(
        "sp,sad->apd", dispatch, returned, preferred_element_type=jnp.float32
    ).astype(jnp.bfloat16)
    outputs = jnp.where(extra[None, :, None], extra_back[:, None, :], combined)
    grad_weight = (weight_grad + extra_wg).astype(jnp.bfloat16)[None]
    grad_bias = (bias_grad + extra_bg)[None]
    return (outputs[0], outputs[1:], grad_weight, grad_bias)


def solution(mesh):
    return jax.shard_map(
        body,
        mesh=mesh,
        in_specs=(
            P(("expert", "helper")),
            P(),
            P(("expert", "helper"), None),
            P(None, ("expert", "helper"), None),
            P(("expert", "helper"), None, None),
            P(("expert", "helper"), None),
            P(("expert", "helper"), None),
            P(None, ("expert", "helper"), None),
        ),
        out_specs=(
            P(("expert", "helper"), None),
            P(None, ("expert", "helper"), None),
            P(("expert", "helper"), None, None),
            P(("expert", "helper"), None),
        ),
        check_vma=False,
    )
```

time: 936 us -> 632 us (0.68)
  blocking collectives: 294 us -> 0 us
  waiting for transfers between devices: 279 us -> 470 us
  local copies, waits for them, and re-layouts: 231 us -> 53 us
  other arithmetic: 73.6 us -> 23 us
  matrix products: 20.1 us -> 37.4 us
  between operations: 1.16 us -> 15.4 us
    all_to_all x2 -> x0, blocking collectives: 294 us -> none  [the longest x1 150 us: body(): lax.all_to_all(arrange(inputs_local), 'expert', split_axis=1, concat_axis...]
    unnamed x0 -> x3, waiting for transfers between devices: none -> 279 us
    all_to_all x4 -> x2, waiting for transfers between devices: 279 us -> 191 us  [the longest x1 191 us: body(): lax.all_to_all(send.reshape(groups, cap * 8, feature_dim), AXES, 0, 0, ti...]
    slice x10 -> x4, local copies, waits for them, and re-layouts: 76.4 us -> 13 us  [the longest x1 9.56 us: body(): received[:, 4:]]
    gather x3 -> x0, local copies, waits for them, and re-layouts: 53.4 us -> none  [the longest x2 48.1 us: arrange(): placed = jnp.take(stacked, source, axis=1, mode='fill', fill_value=0)]
    all_to_all x5 -> x0, local copies, waits for them, and re-layouts: 43.5 us -> none  [the longest x1 10.9 us: body(): lax.all_to_all(lax.all_to_all(arrange(inputs_local), 'expert', split_axis...]
    dot_general x3 -> x8, matrix products: 20.1 us -> 37.4 us  [the longest x2 14.6 us: expert_pass(): lax.dot_general(flat, gradients.reshape(slot_count * depth, feature_dim),...]
    another operation x1 -> x0, local copies, waits for them, and re-layouts: 16.3 us -> none  [forward_pass(): inputs.reshape(4 * slot_count, feature_dim)]
  transfers between devices with their start and end apart: 4 -> 4, of which waited for: 4 -> 2; matrix products, arithmetic and copies ran while one was open for 8% -> 12% of each run, Pallas kernels for 0% -> 0%
where the time goes in v1:
time: 632 us; the launch traced here: 625 us
  waiting for transfers between devices  470 us (74%)
  local copies, waits for them, and re-layouts  53 us (8%)
  matrix products  37.4 us (6%)
  starting transfers between devices  26.2 us (4%)
  other arithmetic  23 us (4%)
  between operations  15.4 us (2%)
    unnamed x3, waiting for transfers between devices  279 us
    all_to_all x1, waiting for transfers between devices, body(): lax.all_to_all(send.reshape(groups, cap * 8, feature_dim), AXES, 0, 0, ti...  191 us
    all_to_all x1, starting transfers between devices, body(): lax.all_to_all(send.reshape(groups, cap * 8, feature_dim), AXES, 0, 0, ti...  16.6 us
    dot_general x2, matrix products, expert_pass(): lax.dot_general(flat, gradients.reshape(slot_count * depth, feature_dim),...  14.6 us
  transfers between devices with their start and end apart: 4, of which 2 were waited for; matrix products, arithmetic and copies ran while one was open for 12% of the time, Pallas kernels for 0%

profile of v1, /device:TPU:1, one launch (start us, length us, event | category | flops | bytes accessed | tf_op | source)
XLA Modules:
  0.0 625.4 jit_solution(11194741618086175010)
XLA Ops:
  7.2 1.1 fusion.35
  9.0 6.1 convolution_convert_fusion
  15.0 11.3 %copy.29 = bf16[512,8,1024]{2,1,0:T(8,128)(2,1)} copy(bf16[512,8,1024]{2,0,1:T(8,128)(2,1)} %convolution_convert_fusion) | data formatting | bytes 16777216 | tf_op jit(solution)/shard_map/convert_element_type | solution.py:73
  26.4 16.6 %all-to-all-start = ((bf16[256,16,1024]{2,1,0:T(8,128)(2,1)}), bf16[256,16,1024]{2,1,0:T(8,128)(2,1)}, u32[]{:S(2)}, u32[]{:S(2)}) async-start(bf16[256,16,1024]{2,1,0:T(8,128)(2,1)} %bitcast.97), calls=%async_computation | async-start | bytes 16777216 | tf_op jit(solution)/shard_map/all_to_all | solution.py:80
  43.6 2.3 fusion.46
  46.5 191.2 %all-to-all-done = bf16[256,16,1024]{2,1,0:T(8,128)(2,1)} async-done(((bf16[256,16,1024]{2,1,0:T(8,128)(2,1)}), bf16[256,16,1024]{2,1,0:T(8,128)(2,1)}, u32[]{:S(2)}, u32[]{:S(2)}) %all-to-all-start) | async-done | bytes 8388640 | tf_op jit(solution)/shard_map/all_to_all | solution.py:80
  237.8 9.6 %fusion.64 = (bf16[512,4,1024]{2,1,0:T(4,128)(2,1)S(1)}, bf16[512,4,1024]{2,1,0:T(4,128)(2,1)S(1)}) fusion(bf16[512,8,1024]{2,1,0:T(8,128)(2,1)} %bitcast.12), kind=kLoop, calls=%fused_computation.92 | loop fusion | bytes 16777216 | tf_op jit(solution)/shard_map/slice | solution.py:87
  247.3 1.5 copy_convert_fusion
  248.8 0.7 copy-done.6
  249.6 5.6 fusion.8
  255.2 1.8 multiply_reduce_fusion
  257.0 2.9 fusion.22
  259.9 3.5 multiply_convert_fusion
  263.8 5.2 copy.31
  269.0 6.9 %reshape.95 = bf16[256,8,1024]{2,1,0:T(8,128)(2,1)} reshape(bf16[512,4,1024]{2,1,0:T(4,128)(2,1)} %copy.31) | data formatting | bytes 8388608 | tf_op jit(solution)/shard_map/reshape | solution.py:94
  275.9 9.0 %all-to-all-start.1 = ((bf16[256,8,1024]{2,1,0:T(8,128)(2,1)}), bf16[256,8,1024]{2,1,0:T(8,128)(2,1)}, u32[]{:S(2)}, u32[]{:S(2)}) async-start(bf16[256,8,1024]{2,1,0:T(8,128)(2,1)} %reshape.95), calls=%async_computation.1 | async-start | bytes 8388608 | tf_op jit(solution)/shard_map/all_to_all | solution.py:93
  286.5 1.7 fusion.65
  289.5 2.6 fusion.24
  292.2 0.8 multiply_reduce_fusion.1
  293.0 1.7 fusion.45
  294.7 2.2 multiply_convert_fusion.2
  297.1 2.9 copy.28
  300.1 2.0 fusion.42
  302.1 279.1 %all-reduce.3.cloned.1.call-done = bf16[256,4,1024]{2,1,0:T(4,128)(2,1)} async-done(((bf16[256,4,1024]{2,1,0:T(4,128)(2,1)}), bf16[256,4,1024]{2,1,0:T(4,128)(2,1)}) %all-reduce.3.cloned.1.call-update) | async-done | bytes 2097168
  581.9 3.8 fusion.19
  586.3 9.4 %fusion = f32[1024,1024,1]{1,0,2:T(8,128)S(1)} fusion(bf16[512,3,1024]{2,0,1:T(8,128)(2,1)} %get-tuple-element.28, bf16[512,1,1024]{2,0,1:T(8,128)(2,1)S(1)} %copy-done.11, bf16[512,4,1024]{2,1,0:T(4,128)(2,1)S(1)} %copy-done.7), kind=kOutput, calls=%fused_computation.7 | convolution fusion | flops 4297064448 | bytes 12582912 | tf_op jit(solution)/shard_map/dot_general | solution.py:41
  595.7 5.2 fusion.30
  600.9 7.2 %reshape.96 = bf16[512,4,1024]{2,1,0:T(4,128)(2,1)} reshape(bf16[256,8,1024]{2,1,0:T(8,128)(2,1)} %all-to-all-done.1) | data formatting | bytes 8388608 | tf_op jit(solution)/shard_map/reshape | solution.py:95
  608.1 5.1 select_bitcast_fusion.1
  613.2 1.3 slice.69
  614.5 2.6 copy.38
  617.1 1.0 copy.37
  (52 shorter events, 6.1 us)
Async XLA Ops:
  7.2 242.4 %copy-start = (bf16[1,1024,1024]{2,1,0:T(8,128)(2,1)S(1)}, bf16[1,1024,1024]{2,1,0:T(8,128)(2,1)}, u32[]{:S(2)}) copy-start(bf16[1,1024,1024]{2,1,0:T(8,128)(2,1)} %param.12) | copy-start | bytes 6291460
  26.4 17.2 %copy-start.14 = (bf16[256,1024]{1,0:T(8,128)(2,1)S(1)}, bf16[256,1024]{1,0:T(8,128)(2,1)}, u32[]{:S(2)}) copy-start(bf16[256,1024]{1,0:T(8,128)(2,1)} %param.14) | copy-start | bytes 1572868
  26.4 17.2 %copy-start.15 = (bf16[256,1024]{1,0:T(8,128)(2,1)S(1)}, bf16[256,1024]{1,0:T(8,128)(2,1)}, u32[]{:S(2)}) copy-start(bf16[256,1024]{1,0:T(8,128)(2,1)} %param.10) | copy-start | bytes 1572868
  26.4 211.4 %all-to-all-start = ((bf16[256,16,1024]{2,1,0:T(8,128)(2,1)}), bf16[256,16,1024]{2,1,0:T(8,128)(2,1)}, u32[]{:S(2)}, u32[]{:S(2)}) async-start(bf16[256,16,1024]{2,1,0:T(8,128)(2,1)} %bitcast.97), calls=%async_computation | async-start | bytes 16777216 | tf_op jit(solution)/shard_map/all_to_all | solution.py:80
  43.0 243.1 %all-gather.3.cloned.1.call-start = ((), (), s32[]{:S(2)}) async-start(), calls=%async_computation.2 | async-start | bytes 4210688 | tf_op jit(solution)/shard_map/all_gather | solution.py:78
  43.6 2.9 copy-start.13
  247.3 2.2 copy-start.6
  248.8 11.1 %copy-start.1 = (f32[512,4,1024]{2,0,1:T(8,128)}, f32[512,4,1024]{2,0,1:T(8,128)S(1)}, u32[]{:S(2)}) copy-start(f32[512,4,1024]{2,0,1:T(8,128)S(1)} %copy_convert_fusion) | copy-start | bytes 25165828
  255.2 4.7 copy-start.3
  257.0 2.9 copy-start.4
  275.9 9.0 %copy-start.16 = (s32[256]{0:T(256)S(1)}, s32[256]{0:T(256)}, u32[]{:S(2)}) copy-start(s32[256]{0:T(256)} %param.9) | copy-start | bytes 3076
  275.9 325.0 %all-to-all-start.1 = ((bf16[256,8,1024]{2,1,0:T(8,128)(2,1)}), bf16[256,8,1024]{2,1,0:T(8,128)(2,1)}, u32[]{:S(2)}, u32[]{:S(2)}) async-start(bf16[256,8,1024]{2,1,0:T(8,128)(2,1)} %reshape.95), calls=%async_computation.1 | async-start | bytes 8388608 | tf_op jit(solution)/shard_map/all_to_all | solution.py:93
  284.9 296.2 %all-reduce.3.cloned.1.call-start = ((), (), s32[]{:S(2)}) async-start(), calls=%async_computation.3 | async-start | bytes 4194304
  288.1 1.4 copy-start.8
  288.9 5.8 copy-start.2
  292.1 2.5 copy-start.5
  581.8 4.4 copy-start.7
  581.8 4.4 copy-start.11
  586.3 9.4 %copy-start.9 = (bf16[256,4,1024]{2,1,0:T(4,128)(2,1)S(1)}, bf16[256,4,1024]{2,1,0:T(4,128)(2,1)}, u32[]{:S(2)}) copy-start(bf16[256,4,1024]{2,1,0:T(4,128)(2,1)} %copy-done.8) | copy-start | bytes 6291460
  586.3 9.4 %copy-start.10 = (bf16[256,3,1024]{2,0,1:T(8,128)(2,1)S(1)}, bf16[256,3,1024]{2,0,1:T(8,128)(2,1)}, u32[]{:S(2)}) copy-start(bf16[256,3,1024]{2,0,1:T(8,128)(2,1)} %get-tuple-element.30) | copy-start | bytes 4718596
  586.3 9.5 %copy-start.12 = (bf16[256,1,1024]{2,0,1:T(8,128)(2,1)S(1)}, bf16[256,1,1024]{2,0,1:T(8,128)(2,1)}, u32[]{:S(2)}) copy-start(bf16[256,1,1024]{2,0,1:T(8,128)(2,1)} %get-tuple-element.23) | copy-start | bytes 1572868
Sparse Core Ops, SparseCore 0:
  48.1 129.5 all-gather.2
  300.2 280.8 all-reduce.2

commit v2 on v1

--- a/solution.py
+++ b/solution.py
@@ -67,15 +67,16 @@
     ).astype(jnp.bfloat16)
     extra = jnp.logical_not(main)
 
-    stacked = jnp.concatenate([features[None], tangents, cot_value[None], cot_tangent], axis=0)
-    send = jnp.einsum(
-        "sp,apd->sad", dispatch, stacked, preferred_element_type=jnp.float32
-    ).astype(jnp.bfloat16)
-    extra_rows = jnp.einsum(
-        "p,apd->ad", extra.astype(jnp.bfloat16), stacked, preferred_element_type=jnp.float32
+    stacked = jnp.concatenate(
+        [features[:, None], tangents.transpose(1, 0, 2), cot_value[:, None], cot_tangent.transpose(1, 0, 2)],
+        axis=1,
+    ).reshape(samples, 8 * feature_dim)
+    send = jnp.dot(dispatch, stacked, preferred_element_type=jnp.float32).astype(jnp.bfloat16)
+    extra_rows = jnp.dot(
+        extra.astype(jnp.bfloat16)[None, :], stacked, preferred_element_type=jnp.float32
     ).astype(jnp.bfloat16)
 
-    gathered = lax.all_gather(extra_rows, AXES, axis=0, tiled=False)
+    gathered = lax.all_gather(extra_rows.reshape(8, feature_dim), AXES, axis=0, tiled=False)
     gathered = jnp.where(is_hot, gathered, jnp.zeros_like(gathered))
     received = lax.all_to_all(
         send.reshape(groups, cap * 8, feature_dim), AXES, 0, 0, tiled=True
@@ -90,14 +91,17 @@
         gathered[:, :4], gathered[:, 4:], weight, bias_row
     )
 
-    returned = lax.all_to_all(
-        results.reshape(groups, cap * 4, feature_dim), AXES, 0, 0, tiled=True
-    ).reshape(groups * cap, 4, feature_dim)
-    extra_results = jnp.where(is_hot, extra_results, jnp.zeros_like(extra_results))
-    extra_back = lax.psum_scatter(extra_results, AXES, scatter_dimension=0, tiled=True)[0]
+    back = jnp.concatenate(
+        [results.reshape(groups, cap, 4, feature_dim), extra_results[:, None]], axis=1
+    ).reshape(groups, (cap + 1) * 4, feature_dim)
+    returned = lax.all_to_all(back, AXES, 0, 0, tiled=True).reshape(groups, cap + 1, 4, feature_dim)
+    extra_back = lax.dynamic_index_in_dim(returned[:, cap], hot_expert[0], axis=0, keepdims=False)
 
     combined = jnp.einsum(
-        "sp,sad->apd", dispatch, returned, preferred_element_type=jnp.float32
+        "sp,sad->apd",
+        dispatch,
+        returned[:, :cap].reshape(groups * cap, 4, feature_dim),
+        preferred_element_type=jnp.float32,
     ).astype(jnp.bfloat16)
     outputs = jnp.where(extra[None, :, None], extra_back[:, None, :], combined)
     grad_weight = (weight_grad + extra_wg).astype(jnp.bfloat16)[None]

time: 632 us -> 526 us (0.83)
  waiting for transfers between devices: 470 us -> 339 us
  local copies, waits for them, and re-layouts: 53 us -> 71.3 us
  other arithmetic: 23 us -> 34.7 us
    unnamed x3 -> x1, waiting for transfers between devices: 279 us -> 0.02 us
    all_to_all x1, waiting for transfers between devices: 0.01 us -> 166 us  [body(): lax.all_to_all(back, AXES, 0, 0, tiled=True)]
    all_to_all x1, waiting for transfers between devices: 191 us -> 43.9 us  [body(): lax.all_to_all(send.reshape(groups, cap * 8, feature_dim), AXES, 0, 0, ti...]
    all_gather x1, waiting for transfers between devices: 0.02 us -> 129 us  [body(): lax.all_gather(extra_rows.reshape(8, feature_dim), AXES, axis=0, tiled=Fa...]
    convert_element_type x1 -> x0, local copies, waits for them, and re-layouts: 11.3 us -> none  [body(): send = jnp.einsum('sp,apd->sad', dispatch, stacked, preferred_element_typ...]
    unnamed x36 -> x45, local copies, waits for them, and re-layouts: 5 us -> 14 us
    concatenate x1 -> x4, local copies, waits for them, and re-layouts: 5.22 us -> 13.5 us  [expert_pass(): results = jnp.concatenate([values[:, None], carried], axis=1)]
    all_to_all x0 -> x1, local copies, waits for them, and re-layouts: none -> 7.1 us  [body(): lax.all_to_all(back, AXES, 0, 0, tiled=True)]
  transfers between devices with their start and end apart: 4 -> 3, of which waited for: 2 -> 3; matrix products, arithmetic and copies ran while one was open for 12% -> 7% of each run, Pallas kernels for 0% -> 0%
where the time goes in v2:
time: 526 us; the launch traced here: 520 us
  waiting for transfers between devices  339 us (64%)
  local copies, waits for them, and re-layouts  71.3 us (14%)
  other arithmetic  34.7 us (7%)
  matrix products  32.1 us (6%)
  starting transfers between devices  26 us (5%)
  between operations  17.2 us (3%)
    all_to_all x1, waiting for transfers between devices, body(): lax.all_to_all(back, AXES, 0, 0, tiled=True)  166 us
    all_gather x1, waiting for transfers between devices, body(): lax.all_gather(extra_rows.reshape(8, feature_dim), AXES, axis=0, tiled=Fa...  129 us
    all_to_all x1, waiting for transfers between devices, body(): lax.all_to_all(send.reshape(groups, cap * 8, feature_dim), AXES, 0, 0, ti...  43.9 us
    all_to_all x1, starting transfers between devices, body(): lax.all_to_all(send.reshape(groups, cap * 8, feature_dim), AXES, 0, 0, ti...  16.6 us
    unnamed x45, local copies, waits for them, and re-layouts  14 us
    reshape x1, local copies, waits for them, and re-layouts, body(): send.reshape(groups, cap * 8, feature_dim)  13.5 us
    concatenate x4, local copies, waits for them, and re-layouts, expert_pass(): results = jnp.concatenate([values[:, None], carried], axis=1)  13.5 us
    dot_general x2, matrix products, expert_pass(): lax.dot_general(flat, gradients.reshape(slot_count * depth, feature_dim),...  10.9 us
  transfers between devices with their start and end apart: 3, of which 3 were waited for; matrix products, arithmetic and copies ran while one was open for 7% of the time, Pallas kernels for 0%

profile of v2, /device:TPU:1, one launch (start us, length us, event | category | flops | bytes accessed | tf_op | source)
XLA Modules:
  0.0 520.3 jit_solution(18206249662721067302)
XLA Ops:
  11.5 2.6 copy.33
  14.1 2.6 copy.35
  16.6 2.1 pad_maximum_fusion.1
  18.8 1.9 copy-done.4
  20.7 5.6 %convolution_convert_fusion = bf16[512,8192]{1,0:T(8,128)(2,1)} fusion(bf16[256,8192]{0,1:T(8,128)(2,1)S(1)} %bitcast.108, s32[256]{0:T(256)S(1)} %multiply_add_fusion, pred[256]{0:T(512)(128)(4,1)S(1)} %get-tuple-element.17), kind=kOutput, calls=%fused_computation | convolution fusion | flops 2151940096 | bytes 12584192 | tf_op jit(solution)/shard_map/dot_general | solution.py:74
  26.4 13.5 %reshape.111 = bf16[256,16,1024]{2,1,0:T(8,128)(2,1)} reshape(bf16[512,8192]{1,0:T(8,128)(2,1)} %convolution_convert_fusion) | data formatting | bytes 16777216 | tf_op jit(solution)/shard_map/reshape | solution.py:82
  39.9 16.6 %all-to-all-start = ((bf16[256,16,1024]{2,1,0:T(8,128)(2,1)}), bf16[256,16,1024]{2,1,0:T(8,128)(2,1)}, u32[]{:S(2)}, u32[]{:S(2)}) async-start(bf16[256,16,1024]{2,1,0:T(8,128)(2,1)} %reshape.111), calls=%async_computation | async-start | bytes 16777216 | tf_op jit(solution)/shard_map/all_to_all | solution.py:81
  56.8 3.4 fusion.58
  62.0 129.2 %all-gather.2.cloned.1.call-done = bf16[256,8,1024]{2,1,0:T(8,128)(2,1)} async-done(((bf16[1,8,1024]{2,1,0:T(8,128)(2,1)}), bf16[256,8,1024]{2,1,0:T(8,128)(2,1)}) %all-gather.2.cloned.1.call-update) | async-done | bytes 4194320 | tf_op jit(solution)/shard_map/all_gather | solution.py:79
  191.2 7.0 %copy_select_fusion = bf16[256,8,1024]{2,0,1:T(8,128)(2,1)S(1)} fusion(bf16[256,8,1024]{2,1,0:T(8,128)(2,1)} %all-gather.2.cloned.1.call-done, pred[]{:T(512)S(6)} %eq.32), kind=kLoop, calls=%fused_computation.16 | loop fusion | flops 2097152 | bytes 8388609 | tf_op jit(solution)/shard_map/jit(_where)/select_n | solution.py:80
  198.7 2.3 fusion.23
  203.6 2.2 multiply_convert_fusion.2
  207.4 43.9 %all-to-all-done = bf16[256,16,1024]{2,1,0:T(8,128)(2,1)} async-done(((bf16[256,16,1024]{2,1,0:T(8,128)(2,1)}), bf16[256,16,1024]{2,1,0:T(8,128)(2,1)}, u32[]{:S(2)}, u32[]{:S(2)}) %all-to-all-start) | async-done | bytes 8388640 | tf_op jit(solution)/shard_map/all_to_all | solution.py:81
  251.3 9.7 %fusion.57 = (bf16[512,4,1024]{2,1,0:T(4,128)(2,1)S(1)}, bf16[512,4,1024]{2,1,0:T(4,128)(2,1)S(1)}) fusion(bf16[512,8,1024]{2,1,0:T(8,128)(2,1)} %bitcast.5), kind=kLoop, calls=%fused_computation.87 | loop fusion | bytes 16777216 | tf_op jit(solution)/shard_map/slice | solution.py:88
  263.3 5.7 %fusion.8 = f32[512,4,1024]{2,0,1:T(8,128)S(1)} fusion(bf16[512,4,1024]{2,1,0:T(4,128)(2,1)S(1)} %get-tuple-element.22, bf16[1,1024,1024]{2,1,0:T(8,128)(2,1)S(1)} %copy-done), kind=kOutput, calls=%fused_computation.18 | convolution fusion | flops 4294967296 | bytes 14680064 | tf_op jit(solution)/shard_map/dot_general | solution.py:26
  270.7 3.3 fusion.22
  274.0 4.3 multiply_convert_fusion
  278.3 2.3 concatenate.24
  280.6 2.5 copy.37
  283.1 5.7 %concatenate.25 = bf16[256,2,3,1024]{3,1,0,2:T(2,128)(2,1)} reshape(bf16[512,3,1024]{2,0,1:T(8,128)(2,1)} %get-tuple-element.27) | data formatting | bytes 6291456 | tf_op jit(solution)/shard_map/concatenate | solution.py:34
  288.8 3.0 copy.38
  292.7 7.0 %copy.40 = bf16[256,12,1024]{2,1,0:T(8,128)(2,1)} copy(bf16[256,12,1024]{2,0,1:T(8,128)(2,1)S(1)} %bitcast.110) | data formatting | bytes 12582912 | tf_op jit(solution)/shard_map/reshape | solution.py:96
  299.7 9.1 %all-to-all-start.1 = ((bf16[256,12,1024]{2,1,0:T(8,128)(2,1)}), bf16[256,12,1024]{2,1,0:T(8,128)(2,1)}, u32[]{:S(2)}, u32[]{:S(2)}) async-start(bf16[256,12,1024]{2,1,0:T(8,128)(2,1)} %copy.40), calls=%async_computation.1 | async-start | bytes 16777216 | tf_op jit(solution)/shard_map/all_to_all | solution.py:97
  310.8 2.1 fusion.38
  312.9 3.8 fusion.19
  317.3 7.0 %fusion = f32[1024,1024,1]{1,0,2:T(8,128)S(1)} fusion(bf16[512,3,1024]{2,0,1:T(8,128)(2,1)S(1)} %copy-done.13, bf16[512,1,1024]{2,0,1:T(8,128)(2,1)S(1)} %copy-done.15, bf16[512,4,1024]{2,1,0:T(4,128)(2,1)S(1)} %copy-done.12), kind=kOutput, calls=%fused_computation.7 | convolution fusion | flops 4297064448 | bytes 12582912 | tf_op jit(solution)/shard_map/dot_general | solution.py:41
  324.4 3.9 fusion.28
  328.2 165.9 %all-to-all-done.1 = bf16[256,12,1024]{2,1,0:T(8,128)(2,1)} async-done(((bf16[256,12,1024]{2,1,0:T(8,128)(2,1)}), bf16[256,12,1024]{2,1,0:T(8,128)(2,1)}, u32[]{:S(2)}, u32[]{:S(2)}) %all-to-all-start.1) | async-done | bytes 6291488 | tf_op jit(solution)/shard_map/all_to_all | solution.py:97
  494.1 7.1 %copy.41 = bf16[256,12,1024]{2,0,1:T(8,128)(2,1)S(1)} copy(bf16[256,12,1024]{2,1,0:T(8,128)(2,1)} %all-to-all-done.1) | data formatting | bytes 12582912 | tf_op jit(solution)/shard_map/all_to_all | solution.py:97
  502.0 3.2 copy.42
  505.2 3.1 select_bitcast_fusion
  509.7 2.6 copy.48
  (64 shorter events, 18.6 us)
Async XLA Ops:
  7.2 191.6 %copy-start = (bf16[1,1024,1024]{2,1,0:T(8,128)(2,1)S(1)}, bf16[1,1024,1024]{2,1,0:T(8,128)(2,1)}, u32[]{:S(2)}) copy-start(bf16[1,1024,1024]{2,1,0:T(8,128)(2,1)} %param.12) | copy-start | bytes 6291460
  18.8 2.0 copy-start.4
  39.9 211.4 %all-to-all-start = ((bf16[256,16,1024]{2,1,0:T(8,128)(2,1)}), bf16[256,16,1024]{2,1,0:T(8,128)(2,1)}, u32[]{:S(2)}, u32[]{:S(2)}) async-start(bf16[256,16,1024]{2,1,0:T(8,128)(2,1)} %reshape.111), calls=%async_computation | async-start | bytes 16777216 | tf_op jit(solution)/shard_map/all_to_all | solution.py:81
  56.5 4.3 copy-start.18
  56.5 4.8 copy-start.17
  56.5 134.7 %all-gather.2.cloned.1.call-start = ((), (), s32[]{:S(2)}) async-start(), calls=%async_computation.2 | async-start | bytes 4210688 | tf_op jit(solution)/shard_map/all_gather | solution.py:79
  198.3 2.8 copy-start.7
  198.7 4.9 copy-start.3
  201.1 2.5 copy-start.6
  261.0 2.2 copy-start.11
  262.5 11.5 %copy-start.2 = (f32[512,4,1024]{2,0,1:T(8,128)}, f32[512,4,1024]{2,0,1:T(8,128)S(1)}, u32[]{:S(2)}) copy-start(f32[512,4,1024]{2,0,1:T(8,128)S(1)} %copy_convert_fusion) | copy-start | bytes 25165828
  268.9 5.1 copy-start.5
  288.8 3.0 copy-start.9
  288.8 3.0 copy-start.10
  299.7 194.4 %all-to-all-start.1 = ((bf16[256,12,1024]{2,1,0:T(8,128)(2,1)}), bf16[256,12,1024]{2,1,0:T(8,128)(2,1)}, u32[]{:S(2)}, u32[]{:S(2)}) async-start(bf16[256,12,1024]{2,1,0:T(8,128)(2,1)} %copy.40), calls=%async_computation.1 | async-start | bytes 16777216 | tf_op jit(solution)/shard_map/all_to_all | solution.py:97
  310.8 6.5 %copy-start.12 = (bf16[512,4,1024]{2,1,0:T(4,128)(2,1)S(1)}, bf16[512,4,1024]{2,1,0:T(4,128)(2,1)}, u32[]{:S(2)}) copy-start(bf16[512,4,1024]{2,1,0:T(4,128)(2,1)} %copy-done.11) | copy-start | bytes 12582916
  310.8 6.5 %copy-start.13 = (bf16[512,3,1024]{2,0,1:T(8,128)(2,1)S(1)}, bf16[512,3,1024]{2,0,1:T(8,128)(2,1)}, u32[]{:S(2)}) copy-start(bf16[512,3,1024]{2,0,1:T(8,128)(2,1)} %get-tuple-element.26) | copy-start | bytes 9437188
  310.8 6.5 %copy-start.15 = (bf16[512,1,1024]{2,0,1:T(8,128)(2,1)S(1)}, bf16[512,1,1024]{2,0,1:T(8,128)(2,1)}, u32[]{:S(2)}) copy-start(bf16[512,1,1024]{2,0,1:T(8,128)(2,1)} %get-tuple-element.18) | copy-start | bytes 3145732
  317.3 7.0 %copy-start.8 = (bf16[256,8,1024]{2,0,1:T(8,128)(2,1)S(1)}, bf16[256,8,1024]{2,0,1:T(8,128)(2,1)}, u32[]{:S(2)}) copy-start(bf16[256,8,1024]{2,0,1:T(8,128)(2,1)} %copy-done.7) | copy-start | bytes 12582916
  317.3 7.0 %copy-start.14 = (bf16[256,3,1024]{2,0,1:T(8,128)(2,1)S(1)}, bf16[256,3,1024]{2,0,1:T(8,128)(2,1)}, u32[]{:S(2)}) copy-start(bf16[256,3,1024]{2,0,1:T(8,128)(2,1)} %get-tuple-element.28) | copy-start | bytes 4718596
  317.3 7.0 %copy-start.16 = (bf16[256,1,1024]{2,0,1:T(8,128)(2,1)S(1)}, bf16[256,1,1024]{2,0,1:T(8,128)(2,1)}, u32[]{:S(2)}) copy-start(bf16[256,1,1024]{2,0,1:T(8,128)(2,1)} %get-tuple-element.23) | copy-start | bytes 1572868
  505.2 8.0 %copy-start.1 = (bf16[1,1024,1024]{2,1,0:T(8,128)(2,1)S(1)}, bf16[1,1024,1024]{2,1,0:T(8,128)(2,1)}, u32[]{:S(2)}) copy-start(bf16[1,1024,1024]{2,1,0:T(8,128)(2,1)} %param.12) | copy-start | bytes 6291460
Sparse Core Ops, SparseCore 0:
  61.6 129.5 all-gather.1

commit v3 on v1

--- a/solution.py
+++ b/solution.py
@@ -58,51 +58,53 @@
     cap = 2 * samples // groups
     me = lax.axis_index("expert") * n_helper + lax.axis_index("helper")
     is_hot = me == hot_expert[0]
+    weight = expert_weight[0]
+    bias_row = expert_bias[0]
 
     rank = ranks_of(route_ids, groups)
-    slot = route_ids * cap + rank
-    main = rank < cap
-    dispatch = (
-        (slot[None, :] == jnp.arange(groups * cap, dtype=jnp.int32)[:, None]) & main[None, :]
-    ).astype(jnp.bfloat16)
-    extra = jnp.logical_not(main)
+    to_expert = route_ids[None, :] == jnp.arange(groups, dtype=jnp.int32)[:, None]
+    extra = rank >= cap
+    stacked = jnp.concatenate([features[None], tangents, cot_value[None], cot_tangent], axis=0)
 
-    stacked = jnp.concatenate([features[None], tangents, cot_value[None], cot_tangent], axis=0)
-    send = jnp.einsum(
-        "sp,apd->sad", dispatch, stacked, preferred_element_type=jnp.float32
-    ).astype(jnp.bfloat16)
+    dispatches = []
+    sends = []
+    for c in range(cap):
+        dispatch = (to_expert & (rank == c)[None, :]).astype(jnp.bfloat16)
+        dispatches.append(dispatch)
+        sends.append(
+            jnp.einsum(
+                "sp,apd->sad", dispatch, stacked, preferred_element_type=jnp.float32
+            ).astype(jnp.bfloat16)
+        )
     extra_rows = jnp.einsum(
         "p,apd->ad", extra.astype(jnp.bfloat16), stacked, preferred_element_type=jnp.float32
     ).astype(jnp.bfloat16)
-
     gathered = lax.all_gather(extra_rows, AXES, axis=0, tiled=False)
     gathered = jnp.where(is_hot, gathered, jnp.zeros_like(gathered))
-    received = lax.all_to_all(
-        send.reshape(groups, cap * 8, feature_dim), AXES, 0, 0, tiled=True
-    ).reshape(groups * cap, 8, feature_dim)
 
-    weight = expert_weight[0]
-    bias_row = expert_bias[0]
-    results, weight_grad, bias_grad = expert_pass(
-        received[:, :4], received[:, 4:], weight, bias_row
-    )
-    extra_results, extra_wg, extra_bg = expert_pass(
+    extra_results, weight_grad, bias_grad = expert_pass(
         gathered[:, :4], gathered[:, 4:], weight, bias_row
     )
+    returned = []
+    for c in range(cap):
+        received = lax.all_to_all(sends[c], AXES, 0, 0, tiled=True)
+        results, slot_wg, slot_bg = expert_pass(received[:, :4], received[:, 4:], weight, bias_row)
+        weight_grad = weight_grad + slot_wg
+        bias_grad = bias_grad + slot_bg
+        if c == 0:
+            results = jnp.concatenate([results, extra_results], axis=1)
+        returned.append(lax.all_to_all(results, AXES, 0, 0, tiled=True))
 
-    returned = lax.all_to_all(
-        results.reshape(groups, cap * 4, feature_dim), AXES, 0, 0, tiled=True
-    ).reshape(groups * cap, 4, feature_dim)
-    extra_results = jnp.where(is_hot, extra_results, jnp.zeros_like(extra_results))
-    extra_back = lax.psum_scatter(extra_results, AXES, scatter_dimension=0, tiled=True)[0]
-
+    extra_back = lax.dynamic_index_in_dim(returned[0][:, 4:], hot_expert[0], axis=0, keepdims=False)
     combined = jnp.einsum(
-        "sp,sad->apd", dispatch, returned, preferred_element_type=jnp.float32
-    ).astype(jnp.bfloat16)
-    outputs = jnp.where(extra[None, :, None], extra_back[:, None, :], combined)
-    grad_weight = (weight_grad + extra_wg).astype(jnp.bfloat16)[None]
-    grad_bias = (bias_grad + extra_bg)[None]
-    return (outputs[0], outputs[1:], grad_weight, grad_bias)
+        "sp,sad->apd", dispatches[0], returned[0][:, :4], preferred_element_type=jnp.float32
+    )
+    for c in range(1, cap):
+        combined = combined + jnp.einsum(
+            "sp,sad->apd", dispatches[c], returned[c], preferred_element_type=jnp.float32
+        )
+    outputs = jnp.where(extra[None, :, None], extra_back[:, None, :], combined.astype(jnp.bfloat16))
+    return (outputs[0], outputs[1:], weight_grad.astype(jnp.bfloat16)[None], bias_grad[None])
 
 
 def solution(mesh):

time: 632 us -> 464 us (0.73)
  waiting for transfers between devices: 470 us -> 280 us
  starting transfers between devices: 26.2 us -> 41.9 us
  local copies, waits for them, and re-layouts: 53 us -> 46.2 us
    unnamed x3 -> x1, waiting for transfers between devices: 279 us -> 0.02 us
    all_to_all x2 -> x4, waiting for transfers between devices: 191 us -> 259 us  [the longest x2 144 us: body(): received = lax.all_to_all(sends[c], AXES, 0, 0, tiled=True)]
    all_gather x1, waiting for transfers between devices: 0.02 us -> 20.7 us  [body(): gathered = lax.all_gather(extra_rows, AXES, axis=0, tiled=False)]
    all_to_all x2 -> x4, starting transfers between devices: 25.6 us -> 41.9 us  [the longest x2 25.5 us: body(): received = lax.all_to_all(sends[c], AXES, 0, 0, tiled=True)]
    reshape x2 -> x0, local copies, waits for them, and re-layouts: 14.1 us -> none  [the longest x1 7.21 us: body(): returned = lax.all_to_all(results.reshape(groups, cap * 4, feature_dim),...]
    dot_general x2 -> x3, matrix products: 14.6 us -> 12.6 us  [expert_pass(): lax.dot_general(flat, gradients.reshape(slot_count * depth, feature_dim),...]
  transfers between devices with their start and end apart: 4 -> 5, of which waited for: 2 -> 5; matrix products, arithmetic and copies ran while one was open for 12% -> 14% of each run, Pallas kernels for 0% -> 0%
where the time goes in v3:
time: 464 us; the launch traced here: 456 us
  waiting for transfers between devices  280 us (60%)
  local copies, waits for them, and re-layouts  46.2 us (10%)
  matrix products  42.4 us (9%)
  starting transfers between devices  41.9 us (9%)
  other arithmetic  28 us (6%)
  between operations  17.3 us (4%)
    all_to_all x2, waiting for transfers between devices, body(): received = lax.all_to_all(sends[c], AXES, 0, 0, tiled=True)  144 us
    all_to_all x2, waiting for transfers between devices, body(): returned.append(lax.all_to_all(results, AXES, 0, 0, tiled=True))  115 us
    all_to_all x2, starting transfers between devices, body(): received = lax.all_to_all(sends[c], AXES, 0, 0, tiled=True)  25.5 us
    all_gather x1, waiting for transfers between devices, body(): gathered = lax.all_gather(extra_rows, AXES, axis=0, tiled=False)  20.7 us
    all_to_all x2, starting transfers between devices, body(): returned.append(lax.all_to_all(results, AXES, 0, 0, tiled=True))  16.4 us
    dot_general x3, matrix products, expert_pass(): lax.dot_general(flat, gradients.reshape(slot_count * depth, feature_dim),...  12.6 us
    dot_general x3, matrix products, expert_pass(): jnp.dot(flat, weight, preferred_element_type=jnp.float32)  11.9 us
    slice x2, local copies, waits for them, and re-layouts, body(): received[:, 4:]  10.9 us
  transfers between devices with their start and end apart: 5, of which 5 were waited for; matrix products, arithmetic and copies ran while one was open for 14% of the time, Pallas kernels for 0%

profile of v3, /device:TPU:1, one launch (start us, length us, event | category | flops | bytes accessed | tf_op | source)
XLA Modules:
  0.0 455.6 jit_solution(6651609676815717496)
XLA Ops:
  8.3 3.4 convolution_convert_fusion
  11.7 4.3 copy.33
  16.1 16.6 %all-to-all-start.2 = ((bf16[256,8,1024]{2,1,0:T(8,128)(2,1)}), bf16[256,8,1024]{2,1,0:T(8,128)(2,1)}, u32[]{:S(2)}, u32[]{:S(2)}) async-start(bf16[256,8,1024]{2,1,0:T(8,128)(2,1)} %copy.33), calls=%async_computation.2 | async-start | bytes 8388608 | tf_op jit(solution)/shard_map/all_to_all | solution.py:90
  35.7 3.1 convolution_convert_fusion.1
  38.9 4.3 copy.28
  43.1 87.6 %all-to-all-done.2 = bf16[256,8,1024]{2,1,0:T(8,128)(2,1)} async-done(((bf16[256,8,1024]{2,1,0:T(8,128)(2,1)}), bf16[256,8,1024]{2,1,0:T(8,128)(2,1)}, u32[]{:S(2)}, u32[]{:S(2)}) %all-to-all-start.2) | async-done | bytes 4194336 | tf_op jit(solution)/shard_map/all_to_all | solution.py:90
  130.8 8.8 %all-to-all-start = ((bf16[256,8,1024]{2,1,0:T(8,128)(2,1)}), bf16[256,8,1024]{2,1,0:T(8,128)(2,1)}, u32[]{:S(2)}, u32[]{:S(2)}) async-start(bf16[256,8,1024]{2,1,0:T(8,128)(2,1)} %copy.28), calls=%async_computation | async-start | bytes 8388608 | tf_op jit(solution)/shard_map/all_to_all | solution.py:90
  140.8 20.7 %all-gather.3.cloned.1.call-done = bf16[2048,1024]{1,0:T(8,128)(2,1)} async-done(((bf16[8,1024]{1,0:T(8,128)(2,1)}), bf16[2048,1024]{1,0:T(8,128)(2,1)}) %all-gather.3.cloned.1.call-update) | async-done | bytes 4194320 | tf_op jit(solution)/shard_map/all_gather | solution.py:82
  163.3 2.7 copy_convert_fusion.2
  166.0 5.2 %fusion.92 = (bf16[256,4,1024]{2,1,0:T(4,128)(2,1)S(1)}, bf16[256,4,1024]{2,1,0:T(4,128)(2,1)S(1)}) fusion(bf16[256,8,1024]{2,1,0:T(8,128)(2,1)} %all-to-all-done.2), kind=kLoop, calls=%fused_computation.133 | loop fusion | bytes 8388608 | tf_op jit(solution)/shard_map/slice | solution.py:91
  171.2 2.7 copy_convert_fusion
  173.9 4.6 %fusion.16 = f32[256,4,1024]{2,0,1:T(8,128)} fusion(bf16[1,1024,1024]{2,1,0:T(8,128)(2,1)S(1)} %copy-done, bf16[256,4,1024]{2,1,0:T(4,128)(2,1)S(1)} %get-tuple-element.29), kind=kOutput, calls=%fused_computation.40 | convolution fusion | flops 2147483648 | bytes 8388608 | tf_op jit(solution)/shard_map/dot_general | solution.py:26
  178.6 4.6 %fusion.14 = f32[256,4,1024]{2,0,1:T(8,128)} fusion(bf16[1,1024,1024]{2,1,0:T(8,128)(2,1)S(1)} %copy-done, bf16[256,4,1024]{2,1,0:T(4,128)(2,1)S(1)} %get-tuple-element.33), kind=kOutput, calls=%fused_computation.38 | convolution fusion | flops 2147483648 | bytes 8388608 | tf_op jit(solution)/shard_map/dot_general | solution.py:26
  183.2 56.5 %all-to-all-done = bf16[256,8,1024]{2,1,0:T(8,128)(2,1)} async-done(((bf16[256,8,1024]{2,1,0:T(8,128)(2,1)}), bf16[256,8,1024]{2,1,0:T(8,128)(2,1)}, u32[]{:S(2)}, u32[]{:S(2)}) %all-to-all-start) | async-done | bytes 4194336 | tf_op jit(solution)/shard_map/all_to_all | solution.py:90
  239.6 5.7 %fusion.91 = (bf16[256,4,1024]{2,1,0:T(4,128)(2,1)S(1)}, bf16[256,4,1024]{2,1,0:T(4,128)(2,1)S(1)}) fusion(bf16[256,8,1024]{2,1,0:T(8,128)(2,1)} %all-to-all-done), kind=kLoop, calls=%fused_computation.132 | loop fusion | bytes 8388608 | tf_op jit(solution)/shard_map/slice | solution.py:91
  248.8 3.0 copy-done.4
  257.4 4.2 fusion.64
  261.6 3.4 multiply_convert_fusion.2
  265.0 4.6 %multiply_convert_fusion = (bf16[256,3,1024]{2,0,1:T(8,128)(2,1)}, bf16[256,3,1024]{2,0,1:T(8,128)(2,1)}, bf16[256,3,1024]{2,0,1:T(8,128)(2,1)S(1)}, bf16[256,3,1024]{2,0,1:T(8,128)(2,1)}) fusion(f32[256,4,1024]{2,0,1:T(8,128)S(1)} %copy-done.2, f32[256,1024]{1,0:T(8,128)} %get-tuple-element.46, f32[256,4,1024]{2,0,1:T(8,128)S(1)} %copy-done.5, ...), kind=kLoop, calls=%fused_computation.7 | loop fusion | flops 6291456 | bytes 20971520 | tf_op jit(solution)/shard_map/convert_element_type | solution.py:39
  270.2 4.3 copy.31
  274.5 8.0 %all-to-all-start.1 = ((bf16[256,8,1024]{2,1,0:T(8,128)(2,1)}), bf16[256,8,1024]{2,1,0:T(8,128)(2,1)}, u32[]{:S(2)}, u32[]{:S(2)}) async-start(bf16[256,8,1024]{2,1,0:T(8,128)(2,1)} %copy.31), calls=%async_computation.1 | async-start | bytes 8388608 | tf_op jit(solution)/shard_map/all_to_all | solution.py:96
  284.2 2.9 copy.35
  287.1 91.7 %all-to-all-done.1 = bf16[256,8,1024]{2,1,0:T(8,128)(2,1)} async-done(((bf16[256,8,1024]{2,1,0:T(8,128)(2,1)}), bf16[256,8,1024]{2,1,0:T(8,128)(2,1)}, u32[]{:S(2)}, u32[]{:S(2)}) %all-to-all-start.1) | async-done | bytes 4194336 | tf_op jit(solution)/shard_map/all_to_all | solution.py:96
  378.8 8.4 %all-to-all-start.3 = ((bf16[256,4,1024]{2,1,0:T(4,128)(2,1)}), bf16[256,4,1024]{2,1,0:T(4,128)(2,1)}, u32[]{:S(2)}, u32[]{:S(2)}) async-start(bf16[256,4,1024]{2,1,0:T(4,128)(2,1)} %copy.35), calls=%async_computation.3 | async-start | bytes 4194304 | tf_op jit(solution)/shard_map/all_to_all | solution.py:96
  389.1 4.1 fusion.49
  393.9 3.7 fusion.1
  397.7 3.7 fusion.5
  401.4 5.2 %fusion.27 = bf16[1,1024,1024]{2,1,0:T(8,128)(2,1)} fusion(bf16[256,3,1024]{2,0,1:T(8,128)(2,1)S(1)} %copy-done.15, bf16[256,1,1024]{2,0,1:T(8,128)(2,1)S(1)} %copy-done.18, bf16[256,4,1024]{2,1,0:T(4,128)(2,1)S(1)} %copy-done.10, f32[1024,1024,1]{1,0,2:T(8,128)S(1)} %fusion.5, f32[1024,1024,1]{1,0,2:T(8,128)S(1)} %fusion.1), kind=kOutput, calls=%fused_computation.52 | convolution fusion | flops 2151677952 | bytes 14680064 | tf_op jit(solution)/shard_map/dot_general | solution.py:41
  406.6 5.7 %fusion.93 = (bf16[256,4,1024]{2,1,0:T(4,128)(2,1)S(1)}, bf16[256,4,1024]{2,1,0:T(4,128)(2,1)S(1)}) fusion(bf16[256,8,1024]{2,1,0:T(8,128)(2,1)} %all-to-all-done.1), kind=kLoop, calls=%fused_computation.134 | loop fusion | bytes 8388608 | tf_op jit(solution)/shard_map/slice | solution.py:98
  412.3 3.6 fusion.12
  416.0 23.3 %all-to-all-done.3 = bf16[256,4,1024]{2,1,0:T(4,128)(2,1)} async-done(((bf16[256,4,1024]{2,1,0:T(4,128)(2,1)}), bf16[256,4,1024]{2,1,0:T(4,128)(2,1)}, u32[]{:S(2)}, u32[]{:S(2)}) %all-to-all-start.3) | async-done | bytes 2097184 | tf_op jit(solution)/shard_map/all_to_all | solution.py:96
  439.3 4.4 select_bitcast_fusion.1
  (75 shorter events, 23.1 us)
Async XLA Ops:
  7.2 166.7 %copy-start = (bf16[1,1024,1024]{2,1,0:T(8,128)(2,1)S(1)}, bf16[1,1024,1024]{2,1,0:T(8,128)(2,1)}, u32[]{:S(2)}) copy-start(bf16[1,1024,1024]{2,1,0:T(8,128)(2,1)} %param.12) | copy-start | bytes 6291460
  16.0 16.7 %copy-start.23 = (bf16[256,1024]{1,0:T(8,128)(2,1)S(1)}, bf16[256,1024]{1,0:T(8,128)(2,1)}, u32[]{:S(2)}) copy-start(bf16[256,1024]{1,0:T(8,128)(2,1)} %param.14) | copy-start | bytes 1572868
  16.0 16.7 %copy-start.24 = (bf16[256,1024]{1,0:T(8,128)(2,1)S(1)}, bf16[256,1024]{1,0:T(8,128)(2,1)}, u32[]{:S(2)}) copy-start(bf16[256,1024]{1,0:T(8,128)(2,1)} %param.10) | copy-start | bytes 1572868
  16.1 114.7 %all-to-all-start.2 = ((bf16[256,8,1024]{2,1,0:T(8,128)(2,1)}), bf16[256,8,1024]{2,1,0:T(8,128)(2,1)}, u32[]{:S(2)}, u32[]{:S(2)}) async-start(bf16[256,8,1024]{2,1,0:T(8,128)(2,1)} %copy.33), calls=%async_computation.2 | async-start | bytes 8388608 | tf_op jit(solution)/shard_map/all_to_all | solution.py:90
  32.7 128.9 %all-gather.3.cloned.1.call-start = ((), (), s32[]{:S(2)}) async-start(), calls=%async_computation.4 | async-start | bytes 4210688 | tf_op jit(solution)/shard_map/all_gather | solution.py:82
  32.8 2.9 copy-start.22
  43.1 96.5 %copy-start.25 = (s32[256]{0:T(256)S(1)}, s32[256]{0:T(256)}, u32[]{:S(2)}) copy-start(s32[256]{0:T(256)} %param.9) | copy-start | bytes 3076
  43.1 97.0 %copy-start.21 = (bf16[1,1024]{1,0:T(2,128)(2,1)S(1)}, bf16[1,1024]{1,0:T(2,128)(2,1)}, u32[]{:S(2)}) copy-start(bf16[1,1024]{1,0:T(2,128)(2,1)} %param.13) | copy-start | bytes 6148
  130.8 108.9 %all-to-all-start = ((bf16[256,8,1024]{2,1,0:T(8,128)(2,1)}), bf16[256,8,1024]{2,1,0:T(8,128)(2,1)}, u32[]{:S(2)}, u32[]{:S(2)}) async-start(bf16[256,8,1024]{2,1,0:T(8,128)(2,1)} %copy.28), calls=%async_computation | async-start | bytes 8388608 | tf_op jit(solution)/shard_map/all_to_all | solution.py:90
  163.3 10.6 %copy-start.11 = (bf16[256,4,1024]{2,1,0:T(4,128)(2,1)}, bf16[256,4,1024]{2,1,0:T(4,128)(2,1)S(1)}, u32[]{:S(2)}) copy-start(bf16[256,4,1024]{2,1,0:T(4,128)(2,1)S(1)} %get-tuple-element.29) | copy-start | bytes 6291460
  171.2 7.3 %copy-start.9 = (bf16[256,4,1024]{2,1,0:T(4,128)(2,1)}, bf16[256,4,1024]{2,1,0:T(4,128)(2,1)S(1)}, u32[]{:S(2)}) copy-start(bf16[256,4,1024]{2,1,0:T(4,128)(2,1)S(1)} %get-tuple-element.33) | copy-start | bytes 6291460
  245.3 2.7 copy-start.13
  245.3 3.4 copy-start.7
  248.0 17.0 %copy-start.6 = (f32[256,4,1024]{2,0,1:T(8,128)}, f32[256,4,1024]{2,0,1:T(8,128)S(1)}, u32[]{:S(2)}) copy-start(f32[256,4,1024]{2,0,1:T(8,128)S(1)} %fusion.18) | copy-start | bytes 12582916
  248.0 3.8 copy-start.4
  248.0 5.2 %copy-start.5 = (f32[256,4,1024]{2,0,1:T(8,128)S(1)}, f32[256,4,1024]{2,0,1:T(8,128)}, u32[]{:S(2)}) copy-start(f32[256,4,1024]{2,0,1:T(8,128)} %fusion.14) | copy-start | bytes 12582916
  251.8 13.2 %copy-start.3 = (f32[256,4,1024]{2,0,1:T(8,128)}, f32[256,4,1024]{2,0,1:T(8,128)S(1)}, u32[]{:S(2)}) copy-start(f32[256,4,1024]{2,0,1:T(8,128)S(1)} %copy_convert_fusion.1) | copy-start | bytes 12582916
  251.8 4.0 copy-start.2
  265.0 4.7 %copy-start.8 = (bf16[256,1,1024]{2,0,1:T(8,128)(2,1)S(1)}, bf16[256,1,1024]{2,0,1:T(8,128)(2,1)}, u32[]{:S(2)}) copy-start(bf16[256,1,1024]{2,0,1:T(8,128)(2,1)} %get-tuple-element.43) | copy-start | bytes 1572868
  274.5 104.3 %all-to-all-start.1 = ((bf16[256,8,1024]{2,1,0:T(8,128)(2,1)}), bf16[256,8,1024]{2,1,0:T(8,128)(2,1)}, u32[]{:S(2)}, u32[]{:S(2)}) async-start(bf16[256,8,1024]{2,1,0:T(8,128)(2,1)} %copy.31), calls=%async_computation.1 | async-start | bytes 8388608 | tf_op jit(solution)/shard_map/all_to_all | solution.py:96
  378.8 60.5 %all-to-all-start.3 = ((bf16[256,4,1024]{2,1,0:T(4,128)(2,1)}), bf16[256,4,1024]{2,1,0:T(4,128)(2,1)}, u32[]{:S(2)}, u32[]{:S(2)}) async-start(bf16[256,4,1024]{2,1,0:T(4,128)(2,1)} %copy.35), calls=%async_computation.3 | async-start | bytes 4194304 | tf_op jit(solution)/shard_map/all_to_all | solution.py:96
  389.1 4.8 %copy-start.12 = (bf16[256,4,1024]{2,1,0:T(4,128)(2,1)S(1)}, bf16[256,4,1024]{2,1,0:T(4,128)(2,1)}, u32[]{:S(2)}) copy-start(bf16[256,4,1024]{2,1,0:T(4,128)(2,1)} %copy-done.11) | copy-start | bytes 6291460
  389.1 4.8 %copy-start.16 = (bf16[256,3,1024]{2,0,1:T(8,128)(2,1)S(1)}, bf16[256,3,1024]{2,0,1:T(8,128)(2,1)}, u32[]{:S(2)}) copy-start(bf16[256,3,1024]{2,0,1:T(8,128)(2,1)} %get-tuple-element.36) | copy-start | bytes 4718596
  389.1 4.8 %copy-start.20 = (bf16[256,1,1024]{2,0,1:T(8,128)(2,1)S(1)}, bf16[256,1,1024]{2,0,1:T(8,128)(2,1)}, u32[]{:S(2)}) copy-start(bf16[256,1,1024]{2,0,1:T(8,128)(2,1)} %get-tuple-element.19) | copy-start | bytes 1572868
  393.9 3.8 copy-start.14
  393.9 3.8 copy-start.17
  393.9 3.8 copy-start.19
  397.7 3.8 copy-start.10
  397.7 3.8 copy-start.15
  397.7 3.8 copy-start.18
  443.7 4.9 %copy-start.1 = (bf16[1,1024,1024]{2,1,0:T(8,128)(2,1)S(1)}, bf16[1,1024,1024]{2,1,0:T(8,128)(2,1)}, u32[]{:S(2)}) copy-start(bf16[1,1024,1024]{2,1,0:T(8,128)(2,1)} %param.12) | copy-start | bytes 6291460
Sparse Core Ops, SparseCore 0:
  37.8 123.7 all-gather.2

commit v4 on v2

--- a/solution.py
+++ b/solution.py
@@ -20,18 +20,21 @@
     return jnp.sum(before * onehot.astype(jnp.float32), axis=1).astype(jnp.int32)
 
 
-def expert_pass(inputs, cotangent, weight, bias_row):
+def forward_pass(inputs, weight, bias_row):
     slot_count, depth, feature_dim = inputs.shape
-    flat = inputs.reshape(slot_count * depth, feature_dim)
-    product = jnp.dot(flat, weight, preferred_element_type=jnp.float32).reshape(
-        slot_count, depth, feature_dim
-    )
+    product = jnp.dot(
+        inputs.reshape(slot_count * depth, feature_dim), weight, preferred_element_type=jnp.float32
+    ).reshape(slot_count, depth, feature_dim)
     preact = product[:, 0] + bias_row[None, :]
     directed = product[:, 1:]
     slopes = jax.nn.sigmoid(preact)
     values = jax.nn.softplus(preact).astype(jnp.bfloat16)
     carried = (slopes[:, None] * directed).astype(jnp.bfloat16)
-    results = jnp.concatenate([values[:, None], carried], axis=1)
+    return jnp.concatenate([values[:, None], carried], axis=1), slopes, directed
+
+
+def backward_pass(inputs, slopes, directed, cotangent):
+    slot_count, depth, feature_dim = inputs.shape
     cot_float = cotangent.astype(jnp.float32)
     grad_pre = cot_float[:, 0] * slopes + jnp.sum(cot_float[:, 1:] * directed, axis=1) * slopes * (
         1.0 - slopes
@@ -39,12 +42,12 @@
     grad_dir = (cot_float[:, 1:] * slopes[:, None]).astype(jnp.bfloat16)
     gradients = jnp.concatenate([grad_pre.astype(jnp.bfloat16)[:, None], grad_dir], axis=1)
     weight_grad = lax.dot_general(
-        flat,
+        inputs.reshape(slot_count * depth, feature_dim),
         gradients.reshape(slot_count * depth, feature_dim),
         (((0,), (0,)), ((), ())),
         preferred_element_type=jnp.float32,
     )
-    return results, weight_grad, jnp.sum(grad_pre, axis=0)
+    return weight_grad, jnp.sum(grad_pre, axis=0)
 
 
 def body(
@@ -58,6 +61,8 @@
     cap = 2 * samples // groups
     me = lax.axis_index("expert") * n_helper + lax.axis_index("helper")
     is_hot = me == hot_expert[0]
+    weight = expert_weight[0]
+    bias_row = expert_bias[0]
 
     rank = ranks_of(route_ids, groups)
     slot = route_ids * cap + rank
@@ -67,36 +72,41 @@
     ).astype(jnp.bfloat16)
     extra = jnp.logical_not(main)
 
-    stacked = jnp.concatenate(
-        [features[:, None], tangents.transpose(1, 0, 2), cot_value[:, None], cot_tangent.transpose(1, 0, 2)],
-        axis=1,
-    ).reshape(samples, 8 * feature_dim)
-    send = jnp.dot(dispatch, stacked, preferred_element_type=jnp.float32).astype(jnp.bfloat16)
-    extra_rows = jnp.dot(
-        extra.astype(jnp.bfloat16)[None, :], stacked, preferred_element_type=jnp.float32
+    def place(stacked):
+        return jnp.einsum(
+            "sp,apd->sad", dispatch, stacked, preferred_element_type=jnp.float32
+        ).astype(jnp.bfloat16).reshape(groups, cap * 4, feature_dim)
+
+    def transfer(stacked):
+        return lax.all_to_all(stacked, AXES, 0, 0, tiled=True).reshape(groups * cap, 4, feature_dim)
+
+    inputs_local = jnp.concatenate([features[None], tangents], axis=0)
+    cot_local = jnp.concatenate([cot_value[None], cot_tangent], axis=0)
+    stacked = jnp.concatenate([inputs_local, cot_local], axis=0)
+    extra_rows = jnp.einsum(
+        "p,apd->ad", extra.astype(jnp.bfloat16), stacked, preferred_element_type=jnp.float32
     ).astype(jnp.bfloat16)
+    gathered = lax.all_gather(extra_rows, AXES, axis=0, tiled=False)
+    gathered = jnp.where(is_hot, gathered, jnp.zeros_like(gathered))
 
-    gathered = lax.all_gather(extra_rows.reshape(8, feature_dim), AXES, axis=0, tiled=False)
-    gathered = jnp.where(is_hot, gathered, jnp.zeros_like(gathered))
-    received = lax.all_to_all(
-        send.reshape(groups, cap * 8, feature_dim), AXES, 0, 0, tiled=True
-    ).reshape(groups * cap, 8, feature_dim)
+    inputs = transfer(place(inputs_local))
+    inputs, cot_send = lax.optimization_barrier((inputs, place(cot_local)))
+    cotangent = transfer(cot_send)
 
-    weight = expert_weight[0]
-    bias_row = expert_bias[0]
-    results, weight_grad, bias_grad = expert_pass(
-        received[:, :4], received[:, 4:], weight, bias_row
-    )
-    extra_results, extra_wg, extra_bg = expert_pass(
-        gathered[:, :4], gathered[:, 4:], weight, bias_row
-    )
-
+    results, slopes, directed = forward_pass(inputs, weight, bias_row)
+    extra_results, extra_slopes, extra_directed = forward_pass(gathered[:, :4], weight, bias_row)
     back = jnp.concatenate(
         [results.reshape(groups, cap, 4, feature_dim), extra_results[:, None]], axis=1
     ).reshape(groups, (cap + 1) * 4, feature_dim)
+    back, slopes, directed, extra_slopes, extra_directed = lax.optimization_barrier(
+        (back, slopes, directed, extra_slopes, extra_directed)
+    )
     returned = lax.all_to_all(back, AXES, 0, 0, tiled=True).reshape(groups, cap + 1, 4, feature_dim)
+
+    weight_grad, bias_grad = backward_pass(inputs, slopes, directed, cotangent)
+    extra_wg, extra_bg = backward_pass(gathered[:, :4], extra_slopes, extra_directed, gathered[:, 4:])
+
     extra_back = lax.dynamic_index_in_dim(returned[:, cap], hot_expert[0], axis=0, keepdims=False)
-
     combined = jnp.einsum(
         "sp,sad->apd",
         dispatch,

time: 526 us -> 479 us (0.911)
  waiting for transfers between devices: 339 us -> 252 us
  local copies, waits for them, and re-layouts: 71.3 us -> 97.7 us
  starting transfers between devices: 26 us -> 34.2 us
    all_gather x1, waiting for transfers between devices: 129 us -> 0.02 us  [body(): gathered = lax.all_gather(extra_rows, AXES, axis=0, tiled=False)]
    all_to_all x1 -> x2, waiting for transfers between devices: 43.9 us -> 122 us  [transfer(): lax.all_to_all(stacked, AXES, 0, 0, tiled=True)]
    all_to_all x1, waiting for transfers between devices: 166 us -> 130 us  [body(): lax.all_to_all(back, AXES, 0, 0, tiled=True)]
    convert_element_type x0 -> x3, local copies, waits for them, and re-layouts: none -> 19.2 us  [the longest x2 10.3 us: place(): return jnp.einsum('sp,apd->sad', dispatch, stacked, preferred_element_typ...]
    optimization_barrier x0 -> x2, local copies, waits for them, and re-layouts: none -> 14.6 us  [the longest x1 7.51 us: body(): inputs, cot_send = lax.optimization_barrier((inputs, place(cot_local)))]
    reduce_sum x4, other arithmetic: 8.41 us -> 17.9 us  [the longest x2 14.1 us: backward_pass(): jnp.sum(cot_float[:, 1:] * directed, axis=1) * slopes * (1.0 - slopes)]
    all_to_all x1 -> x2, starting transfers between devices: 16.6 us -> 25.5 us  [transfer(): lax.all_to_all(stacked, AXES, 0, 0, tiled=True)]
    convert_element_type x8 -> x4, other arithmetic: 13.5 us -> 4.7 us  [the longest x1 2.46 us: backward_pass(): cot_float = cotangent.astype(jnp.float32)]
  transfers between devices with their start and end apart: 3 -> 4, of which waited for: 3 -> 3; matrix products, arithmetic and copies ran while one was open for 7% -> 28% of each run, Pallas kernels for 0% -> 0%
where the time goes in v4:
time: 479 us; the launch traced here: 472 us
  waiting for transfers between devices  252 us (53%)
  local copies, waits for them, and re-layouts  97.7 us (20%)
  other arithmetic  36.2 us (8%)
  matrix products  34.2 us (7%)
  starting transfers between devices  34.2 us (7%)
  between operations  17.2 us (4%)
    all_to_all x1, waiting for transfers between devices, body(): lax.all_to_all(back, AXES, 0, 0, tiled=True)  130 us
    all_to_all x2, waiting for transfers between devices, transfer(): lax.all_to_all(stacked, AXES, 0, 0, tiled=True)  122 us
    all_to_all x2, starting transfers between devices, transfer(): lax.all_to_all(stacked, AXES, 0, 0, tiled=True)  25.5 us
    reduce_sum x2, other arithmetic, backward_pass(): jnp.sum(cot_float[:, 1:] * directed, axis=1) * slopes * (1.0 - slopes)  14.1 us
    reshape x2, local copies, waits for them, and re-layouts, place(): return jnp.einsum('sp,apd->sad', dispatch, stacked, preferred_element_typ...  13.9 us
    dot_general x2, matrix products, backward_pass(): lax.dot_general(inputs.reshape(slot_count * depth, feature_dim), gradient...  13.2 us
    concatenate x4, local copies, waits for them, and re-layouts, forward_pass(): jnp.concatenate([values[:, None], carried], axis=1)  12.9 us
    convert_element_type x2, local copies, waits for them, and re-layouts, place(): return jnp.einsum('sp,apd->sad', dispatch, stacked, preferred_element_typ...  10.3 us
  transfers between devices with their start and end apart: 4, of which 3 were waited for; matrix products, arithmetic and copies ran while one was open for 28% of the time, Pallas kernels for 0%

profile of v4, /device:TPU:1, one launch (start us, length us, event | category | flops | bytes accessed | tf_op | source)
XLA Modules:
  0.0 471.6 jit_solution(12568721767138045572)
XLA Ops:
  9.0 2.8 convolution_convert_fusion.1
  11.8 5.2 %copy.32 = bf16[512,4,1024]{2,1,0:T(4,128)(2,1)} copy(bf16[512,4,1024]{2,0,1:T(8,128)(2,1)S(1)} %convolution_convert_fusion.1) | data formatting | bytes 8388608 | tf_op jit(solution)/shard_map/convert_element_type | solution.py:78
  17.0 7.0 %reshape.98 = bf16[256,8,1024]{2,1,0:T(8,128)(2,1)} reshape(bf16[512,4,1024]{2,1,0:T(4,128)(2,1)} %copy.32) | data formatting | bytes 8388608 | tf_op jit(solution)/shard_map/reshape | solution.py:78
  23.9 16.6 %all-to-all-start = ((bf16[256,8,1024]{2,1,0:T(8,128)(2,1)}), bf16[256,8,1024]{2,1,0:T(8,128)(2,1)}, u32[]{:S(2)}, u32[]{:S(2)}) async-start(bf16[256,8,1024]{2,1,0:T(8,128)(2,1)} %reshape.98), calls=%async_computation | async-start | bytes 8388608 | tf_op jit(solution)/shard_map/all_to_all | solution.py:81
  44.1 2.7 convolution_convert_fusion
  46.8 5.2 %copy.33 = bf16[512,4,1024]{2,1,0:T(4,128)(2,1)} copy(bf16[512,4,1024]{2,0,1:T(8,128)(2,1)S(1)} %convolution_convert_fusion) | data formatting | bytes 8388608 | tf_op jit(solution)/shard_map/convert_element_type | solution.py:78
  51.9 6.9 %reshape.100 = bf16[256,8,1024]{2,1,0:T(8,128)(2,1)} reshape(bf16[512,4,1024]{2,1,0:T(4,128)(2,1)} %copy.33) | data formatting | bytes 8388608 | tf_op jit(solution)/shard_map/reshape | solution.py:78
  58.9 79.8 %all-to-all-done = bf16[256,8,1024]{2,1,0:T(8,128)(2,1)} async-done(((bf16[256,8,1024]{2,1,0:T(8,128)(2,1)}), bf16[256,8,1024]{2,1,0:T(8,128)(2,1)}, u32[]{:S(2)}, u32[]{:S(2)}) %all-to-all-start) | async-done | bytes 4194336 | tf_op jit(solution)/shard_map/all_to_all | solution.py:81
  138.7 7.3 %reshape.99 = bf16[512,4,1024]{2,1,0:T(4,128)(2,1)} reshape(bf16[256,8,1024]{2,1,0:T(8,128)(2,1)} %all-to-all-done) | data formatting | bytes 8388608 | tf_op jit(solution)/shard_map/reshape | solution.py:81
  146.0 8.8 %all-to-all-start.2 = ((bf16[256,8,1024]{2,1,0:T(8,128)(2,1)}), bf16[256,8,1024]{2,1,0:T(8,128)(2,1)}, u32[]{:S(2)}, u32[]{:S(2)}) async-start(bf16[256,8,1024]{2,1,0:T(8,128)(2,1)} %reshape.100), calls=%async_computation.2 | async-start | bytes 8388608 | tf_op jit(solution)/shard_map/all_to_all | solution.py:81
  156.0 7.5 %copy.44 = bf16[512,4,1024]{0,2,1:T(8,128)(2,1)} copy(bf16[512,4,1024]{2,1,0:T(4,128)(2,1)} %reshape.99) | data formatting | bytes 8388608 | tf_op jit(solution)/shard_map/optimization_barrier | solution.py:93
  163.5 6.5 %fusion.36 = f32[512,4,1024]{2,0,1:T(8,128)S(1)} fusion(bf16[512,4,1024]{0,2,1:T(8,128)(2,1)} %copy.44, bf16[1,1024,1024]{2,1,0:T(8,128)(2,1)S(1)} %copy-done), kind=kOutput, calls=%fused_computation.51 | convolution fusion | flops 4294967296 | bytes 14680064 | tf_op jit(solution)/shard_map/dot_general | solution.py:25
  171.5 4.9 %fusion.74 = (f32[512,3,1024]{2,0,1:T(8,128)}, bf16[512,3,1024]{2,0,1:T(8,128)(2,1)}) fusion(f32[512,4,1024]{2,0,1:T(8,128)S(1)} %fusion.36, f32[512,1024]{1,0:T(8,128)S(1)} %get-tuple-element.33), kind=kLoop, calls=%fused_computation.101 | loop fusion | flops 3145728 | bytes 17825792 | tf_op jit(solution)/shard_map/slice | solution.py:29
  176.4 5.7 %concatenate.33 = bf16[256,2,3,1024]{3,1,0,2:T(2,128)(2,1)} reshape(bf16[512,3,1024]{2,0,1:T(8,128)(2,1)} %get-tuple-element.37) | data formatting | bytes 6291456 | tf_op jit(solution)/shard_map/concatenate | solution.py:33
  182.1 4.5 copy.36
  189.6 2.6 fusion.75
  192.3 2.6 fusion.34
  198.4 3.6 fusion.33
  202.8 7.1 %copy.38 = bf16[256,12,1024]{2,1,0:T(8,128)(2,1)} copy(bf16[256,12,1024]{2,0,1:T(8,128)(2,1)S(1)} %bitcast.100) | data formatting | bytes 12582912 | tf_op jit(solution)/shard_map/optimization_barrier | solution.py:101
  209.9 42.4 %all-to-all-done.2 = bf16[256,8,1024]{2,1,0:T(8,128)(2,1)} async-done(((bf16[256,8,1024]{2,1,0:T(8,128)(2,1)}), bf16[256,8,1024]{2,1,0:T(8,128)(2,1)}, u32[]{:S(2)}, u32[]{:S(2)}) %all-to-all-start.2) | async-done | bytes 4194336 | tf_op jit(solution)/shard_map/all_to_all | solution.py:81
  252.3 8.1 %all-to-all-start.1 = ((bf16[256,12,1024]{2,1,0:T(8,128)(2,1)}), bf16[256,12,1024]{2,1,0:T(8,128)(2,1)}, u32[]{:S(2)}, u32[]{:S(2)}) async-start(bf16[256,12,1024]{2,1,0:T(8,128)(2,1)} %copy.38), calls=%async_computation.1 | async-start | bytes 16777216 | tf_op jit(solution)/shard_map/all_to_all | solution.py:104
  267.4 5.8 %fusion.24 = f32[1024,1024,1]{1,0,2:T(8,128)} fusion(bf16[256,3,1024]{2,0,1:T(8,128)(2,1)S(1)} %get-tuple-element.45, bf16[256,1,1024]{2,0,1:T(8,128)(2,1)S(1)} %get-tuple-element.39, bf16[256,4,1024]{2,1,0:T(4,128)(2,1)S(1)} %copy-done.8), kind=kOutput, calls=%fused_computation.36 | convolution fusion | flops 2148532224 | bytes 8388608 | tf_op jit(solution)/shard_map/dot_general | solution.py:44
  273.3 8.8 %reshape.105 = f32[512,4,1024]{2,1,0:T(4,128)} reshape(bf16[256,8,1024]{2,1,0:T(8,128)(2,1)} %all-to-all-done.2) | data formatting | bytes 12582912 | tf_op jit(solution)/shard_map/convert_element_type | solution.py:38
  282.1 8.8 %slice.74 = f32[512,3,1024]{2,1,0:T(4,128)} slice(f32[512,4,1024]{2,1,0:T(4,128)} %reshape.105), slice={[0:512], [1:4], [0:1024]} | slice | bytes 12582912 | tf_op jit(solution)/shard_map/slice | solution.py:39
  290.9 13.1 %multiply_reduce_fusion = (f32[512,1024]{1,0:T(8,128)}, bf16[512,3,1024]{2,0,1:T(8,128)(2,1)}) fusion(f32[512,3,1024]{2,0,1:T(8,128)} %get-tuple-element.15, f32[512,3,1024]{2,1,0:T(4,128)} %slice.74, f32[512,1024]{1,0:T(8,128)} %fusion.33), kind=kLoop, calls=%fused_computation.2 | loop fusion | flops 5767168 | bytes 19922944 | tf_op jit(solution)/shard_map/reduce_sum | solution.py:39
  304.0 3.5 fusion.72
  308.4 7.4 %fusion.42 = bf16[1,1024,1024]{2,1,0:T(8,128)(2,1)} fusion(f32[1024,1024,1]{1,0,2:T(8,128)} %fusion.24, bf16[512,4,1024]{0,2,1:T(8,128)(2,1)S(1)} %copy-done.5, bf16[512,3,1024]{2,0,1:T(8,128)(2,1)S(1)} %copy-done.6, bf16[512,1,1024]{2,0,1:T(8,128)(2,1)S(1)} %get-tuple-element.41), kind=kOutput, calls=%fused_computation.58 | convolution fusion | flops 4299161600 | bytes 14680064 | tf_op jit(solution)/shard_map/dot_general | solution.py:44
  315.8 129.9 %all-to-all-done.1 = bf16[256,12,1024]{2,1,0:T(8,128)(2,1)} async-done(((bf16[256,12,1024]{2,1,0:T(8,128)(2,1)}), bf16[256,12,1024]{2,1,0:T(8,128)(2,1)}, u32[]{:S(2)}, u32[]{:S(2)}) %all-to-all-start.1) | async-done | bytes 6291488 | tf_op jit(solution)/shard_map/all_to_all | solution.py:104
  445.7 6.9 %copy.39 = bf16[256,12,1024]{2,0,1:T(8,128)(2,1)S(1)} copy(bf16[256,12,1024]{2,1,0:T(8,128)(2,1)} %all-to-all-done.1) | data formatting | bytes 12582912 | tf_op jit(solution)/shard_map/all_to_all | solution.py:104
  453.3 3.2 copy.40
  456.6 3.1 select_bitcast_fusion.1
  462.0 2.6 copy.48
  (59 shorter events, 23.6 us)
Async XLA Ops:
  7.2 156.3 %copy-start = (bf16[1,1024,1024]{2,1,0:T(8,128)(2,1)S(1)}, bf16[1,1024,1024]{2,1,0:T(8,128)(2,1)}, u32[]{:S(2)}) copy-start(bf16[1,1024,1024]{2,1,0:T(8,128)(2,1)} %param.12) | copy-start | bytes 6291460
  23.9 17.2 %copy-start.9 = (bf16[256,1024]{1,0:T(8,128)(2,1)S(1)}, bf16[256,1024]{1,0:T(8,128)(2,1)}, u32[]{:S(2)}) copy-start(bf16[256,1024]{1,0:T(8,128)(2,1)} %param.10) | copy-start | bytes 1572868
  23.9 17.3 %copy-start.10 = (bf16[256,1024]{1,0:T(8,128)(2,1)S(1)}, bf16[256,1024]{1,0:T(8,128)(2,1)}, u32[]{:S(2)}) copy-start(bf16[256,1024]{1,0:T(8,128)(2,1)} %param.14) | copy-start | bytes 1572868
  23.9 114.7 %all-to-all-start = ((bf16[256,8,1024]{2,1,0:T(8,128)(2,1)}), bf16[256,8,1024]{2,1,0:T(8,128)(2,1)}, u32[]{:S(2)}, u32[]{:S(2)}) async-start(bf16[256,8,1024]{2,1,0:T(8,128)(2,1)} %reshape.98), calls=%async_computation | async-start | bytes 8388608 | tf_op jit(solution)/shard_map/all_to_all | solution.py:81
  40.6 148.8 %all-gather.3.cloned.1.call-start = ((), (), s32[]{:S(2)}) async-start(), calls=%async_computation.3 | async-start | bytes 4210688 | tf_op jit(solution)/shard_map/all_gather | solution.py:89
  146.0 8.9 %copy-start.12 = (s32[256]{0:T(256)S(1)}, s32[256]{0:T(256)}, u32[]{:S(2)}) copy-start(s32[256]{0:T(256)} %param.9) | copy-start | bytes 3076
  146.0 9.4 %copy-start.11 = (bf16[1,1024]{1,0:T(2,128)(2,1)S(1)}, bf16[1,1024]{1,0:T(2,128)(2,1)}, u32[]{:S(2)}) copy-start(bf16[1,1024]{1,0:T(2,128)(2,1)} %param.13) | copy-start | bytes 6148
  146.0 106.3 %all-to-all-start.2 = ((bf16[256,8,1024]{2,1,0:T(8,128)(2,1)}), bf16[256,8,1024]{2,1,0:T(8,128)(2,1)}, u32[]{:S(2)}, u32[]{:S(2)}) async-start(bf16[256,8,1024]{2,1,0:T(8,128)(2,1)} %reshape.100), calls=%async_computation.2 | async-start | bytes 8388608 | tf_op jit(solution)/shard_map/all_to_all | solution.py:81
  170.0 6.4 %copy-start.2 = (f32[512,4,1024]{2,0,1:T(8,128)}, f32[512,4,1024]{2,0,1:T(8,128)S(1)}, u32[]{:S(2)}) copy-start(f32[512,4,1024]{2,0,1:T(8,128)S(1)} %fusion.36) | copy-start | bytes 25165828
  192.2 2.6 copy-start.7
  198.1 3.9 copy-start.4
  252.3 193.5 %all-to-all-start.1 = ((bf16[256,12,1024]{2,1,0:T(8,128)(2,1)}), bf16[256,12,1024]{2,1,0:T(8,128)(2,1)}, u32[]{:S(2)}, u32[]{:S(2)}) async-start(bf16[256,12,1024]{2,1,0:T(8,128)(2,1)} %copy.38), calls=%async_computation.1 | async-start | bytes 16777216 | tf_op jit(solution)/shard_map/all_to_all | solution.py:104
  262.4 2.5 copy-start.3
  265.8 1.6 copy-start.8
  290.9 13.1 %slice-start = ((f32[512,4,1024]{2,1,0:T(4,128)}), f32[512,1,1024]{2,1,0:T(1,128)S(1)}, s32[]{:S(2)}) async-start(f32[512,4,1024]{2,1,0:T(4,128)} %reshape.105), calls=%async_computation.4 | async-start | bytes 4194304 | tf_op jit(solution)/shard_map/slice | solution.py:39
  304.0 4.1 copy-start.5
  304.0 4.4 copy-start.6
  459.7 4.9 %copy-start.1 = (bf16[1,1024,1024]{2,1,0:T(8,128)(2,1)S(1)}, bf16[1,1024,1024]{2,1,0:T(8,128)(2,1)}, u32[]{:S(2)}) copy-start(bf16[1,1024,1024]{2,1,0:T(8,128)(2,1)} %param.12) | copy-start | bytes 6291460
Sparse Core Ops, SparseCore 0:
  45.7 121.4 all-gather.2

commit v5 on v4

--- a/solution.py
+++ b/solution.py
@@ -95,23 +95,21 @@
 
     results, slopes, directed = forward_pass(inputs, weight, bias_row)
     extra_results, extra_slopes, extra_directed = forward_pass(gathered[:, :4], weight, bias_row)
-    back = jnp.concatenate(
-        [results.reshape(groups, cap, 4, feature_dim), extra_results[:, None]], axis=1
-    ).reshape(groups, (cap + 1) * 4, feature_dim)
-    back, slopes, directed, extra_slopes, extra_directed = lax.optimization_barrier(
-        (back, slopes, directed, extra_slopes, extra_directed)
+    back = results.reshape(groups, cap * 4, feature_dim)
+    back, extra_results, slopes, directed, extra_slopes, extra_directed, cotangent = (
+        lax.optimization_barrier(
+            (back, extra_results, slopes, directed, extra_slopes, extra_directed, cotangent)
+        )
     )
-    returned = lax.all_to_all(back, AXES, 0, 0, tiled=True).reshape(groups, cap + 1, 4, feature_dim)
+    returned = lax.all_to_all(back, AXES, 0, 0, tiled=True).reshape(groups * cap, 4, feature_dim)
+    extra_returned = lax.all_to_all(extra_results, AXES, 0, 0, tiled=True)
 
     weight_grad, bias_grad = backward_pass(inputs, slopes, directed, cotangent)
     extra_wg, extra_bg = backward_pass(gathered[:, :4], extra_slopes, extra_directed, gathered[:, 4:])
 
-    extra_back = lax.dynamic_index_in_dim(returned[:, cap], hot_expert[0], axis=0, keepdims=False)
+    extra_back = lax.dynamic_index_in_dim(extra_returned, hot_expert[0], axis=0, keepdims=False)
     combined = jnp.einsum(
-        "sp,sad->apd",
-        dispatch,
-        returned[:, :cap].reshape(groups * cap, 4, feature_dim),
-        preferred_element_type=jnp.float32,
+        "sp,sad->apd", dispatch, returned, preferred_element_type=jnp.float32
     ).astype(jnp.bfloat16)
     outputs = jnp.where(extra[None, :, None], extra_back[:, None, :], combined)
     grad_weight = (weight_grad + extra_wg).astype(jnp.bfloat16)[None]

time: 479 us -> 458 us (0.956)
  blocking collectives: 0 us -> 59.6 us
  waiting for transfers between devices: 252 us -> 194 us
  local copies, waits for them, and re-layouts: 97.7 us -> 79.9 us
    all_to_all x1, waiting for transfers between devices: 130 us -> 63.8 us  [body(): lax.all_to_all(back, AXES, 0, 0, tiled=True)]
    all_to_all x0 -> x1, blocking collectives: none -> 59.6 us  [body(): extra_returned = lax.all_to_all(extra_results, AXES, 0, 0, tiled=True)]
    reshape x0 -> x2, local copies, waits for them, and re-layouts: none -> 14.3 us  [the longest x1 7.38 us: body(): lax.all_to_all(back, AXES, 0, 0, tiled=True)]
    slice x6 -> x0, local copies, waits for them, and re-layouts: 12.7 us -> none  [the longest x1 8.78 us: backward_pass(): cot_float[:, 1:] * directed]
    convert_element_type x1 -> x0, local copies, waits for them, and re-layouts: 8.8 us -> none  [backward_pass(): cot_float = cotangent.astype(jnp.float32)]
    concatenate x4 -> x1, local copies, waits for them, and re-layouts: 12.9 us -> 5.2 us  [forward_pass(): jnp.concatenate([values[:, None], carried], axis=1)]
    all_to_all x2, waiting for transfers between devices: 122 us -> 130 us  [transfer(): lax.all_to_all(stacked, AXES, 0, 0, tiled=True)]
    reshape x1 -> x2, local copies, waits for them, and re-layouts: 7.29 us -> 14.4 us  [transfer(): lax.all_to_all(stacked, AXES, 0, 0, tiled=True)]
  transfers between devices with their start and end apart: 4 -> 4, of which waited for: 3 -> 3; matrix products, arithmetic and copies ran while one was open for 28% -> 22% of each run, Pallas kernels for 0% -> 0%
where the time goes in v5:
time: 458 us; the launch traced here: 451 us
  waiting for transfers between devices  194 us (42%)
  local copies, waits for them, and re-layouts  79.9 us (17%)
  blocking collectives  59.6 us (13%)
  other arithmetic  34.7 us (8%)
  starting transfers between devices  34.2 us (7%)
  matrix products  32.2 us (7%)
  between operations  17.1 us (4%)
    all_to_all x2, waiting for transfers between devices, transfer(): lax.all_to_all(stacked, AXES, 0, 0, tiled=True)  130 us
    all_to_all x1, waiting for transfers between devices, body(): lax.all_to_all(back, AXES, 0, 0, tiled=True)  63.8 us
    all_to_all x1, blocking collectives, body(): extra_returned = lax.all_to_all(extra_results, AXES, 0, 0, tiled=True)  59.6 us
    all_to_all x2, starting transfers between devices, transfer(): lax.all_to_all(stacked, AXES, 0, 0, tiled=True)  25.6 us
    reshape x2, local copies, waits for them, and re-layouts, transfer(): lax.all_to_all(stacked, AXES, 0, 0, tiled=True)  14.4 us
    reshape x2, local copies, waits for them, and re-layouts, place(): return jnp.einsum('sp,apd->sad', dispatch, stacked, preferred_element_typ...  13.8 us
    convert_element_type x2, local copies, waits for them, and re-layouts, place(): return jnp.einsum('sp,apd->sad', dispatch, stacked, preferred_element_typ...  10.4 us
    dot_general x2, matrix products, backward_pass(): lax.dot_general(inputs.reshape(slot_count * depth, feature_dim), gradient...  9.23 us
  transfers between devices with their start and end apart: 4, of which 3 were waited for; matrix products, arithmetic and copies ran while one was open for 22% of the time, Pallas kernels for 0%

profile of v5, /device:TPU:1, one launch (start us, length us, event | category | flops | bytes accessed | tf_op | source)
XLA Modules:
  0.0 451.4 jit_solution(7115156375606634047)
XLA Ops:
  9.0 2.8 convolution_convert_fusion.1
  11.8 5.2 %copy.28 = bf16[512,4,1024]{2,1,0:T(4,128)(2,1)} copy(bf16[512,4,1024]{2,0,1:T(8,128)(2,1)S(1)} %convolution_convert_fusion.1) | data formatting | bytes 8388608 | tf_op jit(solution)/shard_map/convert_element_type | solution.py:78
  17.0 6.9 %reshape.90 = bf16[256,8,1024]{2,1,0:T(8,128)(2,1)} reshape(bf16[512,4,1024]{2,1,0:T(4,128)(2,1)} %copy.28) | data formatting | bytes 8388608 | tf_op jit(solution)/shard_map/reshape | solution.py:78
  23.9 16.6 %all-to-all-start = ((bf16[256,8,1024]{2,1,0:T(8,128)(2,1)}), bf16[256,8,1024]{2,1,0:T(8,128)(2,1)}, u32[]{:S(2)}, u32[]{:S(2)}) async-start(bf16[256,8,1024]{2,1,0:T(8,128)(2,1)} %reshape.90), calls=%async_computation | async-start | bytes 8388608 | tf_op jit(solution)/shard_map/all_to_all | solution.py:81
  43.8 2.7 convolution_convert_fusion
  46.4 5.2 %copy.29 = bf16[512,4,1024]{2,1,0:T(4,128)(2,1)} copy(bf16[512,4,1024]{2,0,1:T(8,128)(2,1)S(1)} %convolution_convert_fusion) | data formatting | bytes 8388608 | tf_op jit(solution)/shard_map/convert_element_type | solution.py:78
  51.7 6.9 %reshape.92 = bf16[256,8,1024]{2,1,0:T(8,128)(2,1)} reshape(bf16[512,4,1024]{2,1,0:T(4,128)(2,1)} %copy.29) | data formatting | bytes 8388608 | tf_op jit(solution)/shard_map/reshape | solution.py:78
  58.6 80.0 %all-to-all-done = bf16[256,8,1024]{2,1,0:T(8,128)(2,1)} async-done(((bf16[256,8,1024]{2,1,0:T(8,128)(2,1)}), bf16[256,8,1024]{2,1,0:T(8,128)(2,1)}, u32[]{:S(2)}, u32[]{:S(2)}) %all-to-all-start) | async-done | bytes 4194336 | tf_op jit(solution)/shard_map/all_to_all | solution.py:81
  138.6 7.2 %reshape.91 = bf16[512,4,1024]{2,1,0:T(4,128)(2,1)} reshape(bf16[256,8,1024]{2,1,0:T(8,128)(2,1)} %all-to-all-done) | data formatting | bytes 8388608 | tf_op jit(solution)/shard_map/reshape | solution.py:81
  145.9 8.9 %all-to-all-start.1 = ((bf16[256,8,1024]{2,1,0:T(8,128)(2,1)}), bf16[256,8,1024]{2,1,0:T(8,128)(2,1)}, u32[]{:S(2)}, u32[]{:S(2)}) async-start(bf16[256,8,1024]{2,1,0:T(8,128)(2,1)} %reshape.92), calls=%async_computation.1 | async-start | bytes 8388608 | tf_op jit(solution)/shard_map/all_to_all | solution.py:81
  156.0 7.6 %copy.36 = bf16[512,4,1024]{0,2,1:T(8,128)(2,1)} copy(bf16[512,4,1024]{2,1,0:T(4,128)(2,1)} %reshape.91) | data formatting | bytes 8388608 | tf_op jit(solution)/shard_map/optimization_barrier | solution.py:93
  163.6 6.5 %fusion.36 = f32[512,4,1024]{2,0,1:T(8,128)S(1)} fusion(bf16[512,4,1024]{0,2,1:T(8,128)(2,1)} %copy.36, bf16[1,1024,1024]{2,1,0:T(8,128)(2,1)S(1)} %copy-done), kind=kOutput, calls=%fused_computation.52 | convolution fusion | flops 4294967296 | bytes 14680064 | tf_op jit(solution)/shard_map/dot_general | solution.py:25
  171.5 4.0 fusion.74
  176.0 5.2 %copy.31 = bf16[512,4,1024]{2,1,0:T(4,128)(2,1)} copy(bf16[512,4,1024]{2,0,1:T(8,128)(2,1)S(1)} %pad_maximum_fusion) | data formatting | bytes 8388608 | tf_op jit(solution)/shard_map/concatenate | solution.py:33
  181.2 6.9 %reshape.93 = bf16[256,8,1024]{2,1,0:T(8,128)(2,1)} reshape(bf16[512,4,1024]{2,1,0:T(4,128)(2,1)} %copy.31) | data formatting | bytes 8388608 | tf_op jit(solution)/shard_map/reshape | solution.py:98
  188.3 2.9 fusion.75
  192.5 2.6 fusion.34
  195.9 2.5 fusion.76
  202.4 49.8 %all-to-all-done.1 = bf16[256,8,1024]{2,1,0:T(8,128)(2,1)} async-done(((bf16[256,8,1024]{2,1,0:T(8,128)(2,1)}), bf16[256,8,1024]{2,1,0:T(8,128)(2,1)}, u32[]{:S(2)}, u32[]{:S(2)}) %all-to-all-start.1) | async-done | bytes 4194336 | tf_op jit(solution)/shard_map/all_to_all | solution.py:81
  252.2 7.2 %reshape.94 = bf16[512,4,1024]{2,1,0:T(4,128)(2,1)} reshape(bf16[256,8,1024]{2,1,0:T(8,128)(2,1)} %all-to-all-done.1) | data formatting | bytes 8388608 | tf_op jit(solution)/shard_map/reshape | solution.py:81
  259.4 3.2 copy.33
  262.6 59.6 %all_to_all.20 = bf16[256,4,1024]{2,1,0:T(4,128)(2,1)} all-to-all(bf16[256,4,1024]{2,1,0:T(4,128)(2,1)S(1)} %copy.33), channel_id=1, replica_groups=mesh['expert'=32,'helper'=8] {'expert','helper'}, dimensions={0} | all-to-all | bytes 4194304 | tf_op jit(solution)/shard_map/all_to_all | solution.py:105
  322.2 8.4 %all-to-all-start.3 = ((bf16[256,8,1024]{2,1,0:T(8,128)(2,1)}), bf16[256,8,1024]{2,1,0:T(8,128)(2,1)}, u32[]{:S(2)}, u32[]{:S(2)}) async-start(bf16[256,8,1024]{2,1,0:T(8,128)(2,1)} %reshape.93), calls=%async_computation.3 | async-start | bytes 8388608 | tf_op jit(solution)/shard_map/all_to_all | solution.py:104
  338.4 4.7 %copy_convert_fusion = f32[512,4,1024]{2,0,1:T(8,128)} fusion(bf16[512,4,1024]{2,1,0:T(4,128)(2,1)S(1)} %copy-done.2), kind=kLoop, calls=%fused_computation.19 | loop fusion | flops 2097152 | bytes 12582912 | tf_op jit(solution)/shard_map/convert_element_type | solution.py:38
  343.2 7.0 %multiply_reduce_fusion = (f32[512,1024]{1,0:T(8,128)S(1)}, bf16[512,3,1024]{2,0,1:T(8,128)(2,1)S(1)}) fusion(f32[512,3,1024]{2,0,1:T(8,128)} %get-tuple-element.19, f32[512,4,1024]{2,0,1:T(8,128)} %copy_convert_fusion, f32[512,1024]{1,0:T(8,128)S(1)} %fusion.33), kind=kLoop, calls=%fused_computation.1 | loop fusion | flops 5767168 | bytes 19922944 | tf_op jit(solution)/shard_map/reduce_sum | solution.py:39
  350.2 2.5 fusion.72
  353.3 3.6 fusion.26
  356.9 5.7 %fusion.42 = bf16[1,1024,1024]{2,1,0:T(8,128)(2,1)} fusion(f32[1024,1024,1]{1,0,2:T(8,128)S(1)} %fusion.26, bf16[512,4,1024]{0,2,1:T(8,128)(2,1)S(1)} %copy-done.5, bf16[512,3,1024]{2,0,1:T(8,128)(2,1)S(1)} %get-tuple-element.41, bf16[512,1,1024]{2,0,1:T(8,128)(2,1)S(1)} %get-tuple-element.37), kind=kOutput, calls=%fused_computation.59 | convolution fusion | flops 4299161600 | bytes 14680064 | tf_op jit(solution)/shard_map/dot_general | solution.py:44
  363.2 63.8 %all-to-all-done.3 = bf16[256,8,1024]{2,1,0:T(8,128)(2,1)} async-done(((bf16[256,8,1024]{2,1,0:T(8,128)(2,1)}), bf16[256,8,1024]{2,1,0:T(8,128)(2,1)}, u32[]{:S(2)}, u32[]{:S(2)}) %all-to-all-start.3) | async-done | bytes 4194336 | tf_op jit(solution)/shard_map/all_to_all | solution.py:104
  427.0 7.4 %reshape.95 = bf16[512,4,1024]{2,1,0:T(4,128)(2,1)} reshape(bf16[256,8,1024]{2,1,0:T(8,128)(2,1)} %all-to-all-done.3) | data formatting | bytes 8388608 | tf_op jit(solution)/shard_map/reshape | solution.py:104
  434.4 5.1 %select_bitcast_fusion.1 = bf16[4,256,1024]{1,2,0:T(8,128)(2,1)S(1)} fusion(pred[256]{0:T(512)(128)(4,1)S(1)} %get-tuple-element.34, bf16[512,4,1024]{2,1,0:T(4,128)(2,1)} %reshape.95, bf16[4,1024]{1,0:T(4,128)(2,1)S(1)} %dynamic-slice_bitcast_fusion, s32[256]{0:T(256)S(1)} %multiply_add_fusion, pred[256]{0:T(512)(128)(4,1)S(1)} %get-tuple-element.35), kind=kOutput, calls=%fused_computation.54 | convolution fusion | flops 1076101120 | bytes 6301184 | tf_op jit(solution)/shard_map/sp,sad->apd/dot_general | solution.py:111
  440.8 2.6 copy.40
  (54 shorter events, 23.2 us)
Async XLA Ops:
  7.2 156.4 %copy-start = (bf16[1,1024,1024]{2,1,0:T(8,128)(2,1)S(1)}, bf16[1,1024,1024]{2,1,0:T(8,128)(2,1)}, u32[]{:S(2)}) copy-start(bf16[1,1024,1024]{2,1,0:T(8,128)(2,1)} %param.12) | copy-start | bytes 6291460
  23.9 16.9 %copy-start.10 = (bf16[256,1024]{1,0:T(8,128)(2,1)S(1)}, bf16[256,1024]{1,0:T(8,128)(2,1)}, u32[]{:S(2)}) copy-start(bf16[256,1024]{1,0:T(8,128)(2,1)} %param.10) | copy-start | bytes 1572868
  23.9 16.9 %copy-start.11 = (bf16[256,1024]{1,0:T(8,128)(2,1)S(1)}, bf16[256,1024]{1,0:T(8,128)(2,1)}, u32[]{:S(2)}) copy-start(bf16[256,1024]{1,0:T(8,128)(2,1)} %param.14) | copy-start | bytes 1572868
  23.9 114.7 %all-to-all-start = ((bf16[256,8,1024]{2,1,0:T(8,128)(2,1)}), bf16[256,8,1024]{2,1,0:T(8,128)(2,1)}, u32[]{:S(2)}, u32[]{:S(2)}) async-start(bf16[256,8,1024]{2,1,0:T(8,128)(2,1)} %reshape.90), calls=%async_computation | async-start | bytes 8388608 | tf_op jit(solution)/shard_map/all_to_all | solution.py:81
  40.6 147.5 %all-gather.3.cloned.1.call-start = ((), (), s32[]{:S(2)}) async-start(), calls=%async_computation.4 | async-start | bytes 4210688 | tf_op jit(solution)/shard_map/all_gather | solution.py:89
  145.9 9.0 %copy-start.12 = (bf16[1,1024]{1,0:T(2,128)(2,1)S(1)}, bf16[1,1024]{1,0:T(2,128)(2,1)}, u32[]{:S(2)}) copy-start(bf16[1,1024]{1,0:T(2,128)(2,1)} %param.13) | copy-start | bytes 6148
  145.9 9.0 %copy-start.13 = (s32[256]{0:T(256)S(1)}, s32[256]{0:T(256)}, u32[]{:S(2)}) copy-start(s32[256]{0:T(256)} %param.9) | copy-start | bytes 3076
  145.9 106.3 %all-to-all-start.1 = ((bf16[256,8,1024]{2,1,0:T(8,128)(2,1)}), bf16[256,8,1024]{2,1,0:T(8,128)(2,1)}, u32[]{:S(2)}, u32[]{:S(2)}) async-start(bf16[256,8,1024]{2,1,0:T(8,128)(2,1)} %reshape.92), calls=%async_computation.1 | async-start | bytes 8388608 | tf_op jit(solution)/shard_map/all_to_all | solution.py:81
  170.0 5.5 %copy-start.3 = (f32[512,4,1024]{2,0,1:T(8,128)}, f32[512,4,1024]{2,0,1:T(8,128)S(1)}, u32[]{:S(2)}) copy-start(f32[512,4,1024]{2,0,1:T(8,128)S(1)} %fusion.36) | copy-start | bytes 25165828
  191.2 1.3 copy-start.6
  322.2 104.8 %all-to-all-start.3 = ((bf16[256,8,1024]{2,1,0:T(8,128)(2,1)}), bf16[256,8,1024]{2,1,0:T(8,128)(2,1)}, u32[]{:S(2)}, u32[]{:S(2)}) async-start(bf16[256,8,1024]{2,1,0:T(8,128)(2,1)} %reshape.93), calls=%async_computation.3 | async-start | bytes 8388608 | tf_op jit(solution)/shard_map/all_to_all | solution.py:104
  332.5 2.5 copy-start.4
  335.1 3.4 copy-start.2
  350.1 3.2 copy-start.7
  350.1 3.2 copy-start.8
  350.1 3.1 copy-start.9
  353.3 3.6 copy-start.5
  439.4 4.9 %copy-start.1 = (bf16[1,1024,1024]{2,1,0:T(8,128)(2,1)S(1)}, bf16[1,1024,1024]{2,1,0:T(8,128)(2,1)}, u32[]{:S(2)}) copy-start(bf16[1,1024,1024]{2,1,0:T(8,128)(2,1)} %param.12) | copy-start | bytes 6291460
Sparse Core Ops, SparseCore 0:
  45.6 121.3 all-gather.2

commit v6 on v4

--- a/solution.py
+++ b/solution.py
@@ -77,9 +77,6 @@
             "sp,apd->sad", dispatch, stacked, preferred_element_type=jnp.float32
         ).astype(jnp.bfloat16).reshape(groups, cap * 4, feature_dim)
 
-    def transfer(stacked):
-        return lax.all_to_all(stacked, AXES, 0, 0, tiled=True).reshape(groups * cap, 4, feature_dim)
-
     inputs_local = jnp.concatenate([features[None], tangents], axis=0)
     cot_local = jnp.concatenate([cot_value[None], cot_tangent], axis=0)
     stacked = jnp.concatenate([inputs_local, cot_local], axis=0)
@@ -89,19 +86,21 @@
     gathered = lax.all_gather(extra_rows, AXES, axis=0, tiled=False)
     gathered = jnp.where(is_hot, gathered, jnp.zeros_like(gathered))
 
-    inputs = transfer(place(inputs_local))
-    inputs, cot_send = lax.optimization_barrier((inputs, place(cot_local)))
-    cotangent = transfer(cot_send)
+    received = lax.all_to_all(place(inputs_local), AXES, 0, 0, tiled=True)
+    received, cot_send = lax.optimization_barrier((received, place(cot_local)))
+    cot_received = lax.all_to_all(cot_send, AXES, 0, 0, tiled=True)
+    inputs = received.reshape(groups * cap, 4, feature_dim)
 
     results, slopes, directed = forward_pass(inputs, weight, bias_row)
     extra_results, extra_slopes, extra_directed = forward_pass(gathered[:, :4], weight, bias_row)
     back = jnp.concatenate(
         [results.reshape(groups, cap, 4, feature_dim), extra_results[:, None]], axis=1
-    ).reshape(groups, (cap + 1) * 4, feature_dim)
-    back, slopes, directed, extra_slopes, extra_directed = lax.optimization_barrier(
-        (back, slopes, directed, extra_slopes, extra_directed)
     )
-    returned = lax.all_to_all(back, AXES, 0, 0, tiled=True).reshape(groups, cap + 1, 4, feature_dim)
+    back, slopes, directed, extra_slopes, extra_directed, cot_received = lax.optimization_barrier(
+        (back, slopes, directed, extra_slopes, extra_directed, cot_received)
+    )
+    returned = lax.all_to_all(back, AXES, 0, 0, tiled=True)
+    cotangent = cot_received.reshape(groups * cap, 4, feature_dim)
 
     weight_grad, bias_grad = backward_pass(inputs, slopes, directed, cotangent)
     extra_wg, extra_bg = backward_pass(gathered[:, :4], extra_slopes, extra_directed, gathered[:, 4:])

time: 479 us -> 431 us (0.90)
  waiting for transfers between devices: 252 us -> 192 us
  other arithmetic: 36.2 us -> 51.1 us
  local copies, waits for them, and re-layouts: 97.7 us -> 88.6 us
  starting transfers between devices: 34.2 us -> 41.3 us
    all_to_all x3, waiting for transfers between devices: 252 us -> 182 us  [the longest x1 80.3 us: body(): received = lax.all_to_all(place(inputs_local), AXES, 0, 0, tiled=True)]
    optimization_barrier x2 -> x0, local copies, waits for them, and re-layouts: 14.6 us -> none  [the longest x1 7.51 us: body(): inputs, cot_send = lax.optimization_barrier((inputs, place(cot_local)))]
    all_gather x1, waiting for transfers between devices: 0.02 us -> 10.3 us  [body(): gathered = lax.all_gather(extra_rows, AXES, axis=0, tiled=False)]
    all_to_all x3, starting transfers between devices: 33.6 us -> 41.3 us  [the longest x1 17.3 us: body(): cot_received = lax.all_to_all(cot_send, AXES, 0, 0, tiled=True)]
    dot_general x0 -> x1, local copies, waits for them, and re-layouts: none -> 7.16 us  [forward_pass(): jnp.dot(inputs.reshape(slot_count * depth, feature_dim), weight, preferre...]
    all_to_all x1 -> x0, local copies, waits for them, and re-layouts: 6.89 us -> none  [body(): lax.all_to_all(back, AXES, 0, 0, tiled=True)]
    concatenate x4 -> x2, local copies, waits for them, and re-layouts: 12.9 us -> 6.24 us  [forward_pass(): jnp.concatenate([values[:, None], carried], axis=1)]
    concatenate x1, other arithmetic: 0.83 us -> 6.7 us  [body(): jnp.concatenate([results.reshape(groups, cap, 4, feature_dim), extra_resu...]
  transfers between devices with their start and end apart: 4 -> 4, of which waited for: 3 -> 4; matrix products, arithmetic and copies ran while one was open for 28% -> 33% of each run, Pallas kernels for 0% -> 0%
where the time goes in v6:
time: 431 us; the launch traced here: 424 us
  waiting for transfers between devices  192 us (45%)
  local copies, waits for them, and re-layouts  88.6 us (21%)
  other arithmetic  51.1 us (12%)
  starting transfers between devices  41.3 us (10%)
  matrix products  34.3 us (8%)
  between operations  17.1 us (4%)
    all_to_all x1, waiting for transfers between devices, body(): received = lax.all_to_all(place(inputs_local), AXES, 0, 0, tiled=True)  80.3 us
    all_to_all x1, waiting for transfers between devices, body(): returned = lax.all_to_all(back, AXES, 0, 0, tiled=True)  72.6 us
    all_to_all x1, waiting for transfers between devices, body(): cot_received = lax.all_to_all(cot_send, AXES, 0, 0, tiled=True)  28.7 us
    all_to_all x1, starting transfers between devices, body(): cot_received = lax.all_to_all(cot_send, AXES, 0, 0, tiled=True)  17.3 us
    reduce_sum x2, other arithmetic, backward_pass(): jnp.sum(cot_float[:, 1:] * directed, axis=1) * slopes * (1.0 - slopes)  17.1 us
    all_to_all x1, starting transfers between devices, body(): received = lax.all_to_all(place(inputs_local), AXES, 0, 0, tiled=True)  16.6 us
    reshape x2, local copies, waits for them, and re-layouts, place(): return jnp.einsum('sp,apd->sad', dispatch, stacked, preferred_element_typ...  13.8 us
    dot_general x2, matrix products, backward_pass(): lax.dot_general(inputs.reshape(slot_count * depth, feature_dim), gradient...  11.5 us
  transfers between devices with their start and end apart: 4, of which 4 were waited for; matrix products, arithmetic and copies ran while one was open for 33% of the time, Pallas kernels for 0%

profile of v6, /device:TPU:1, one launch (start us, length us, event | category | flops | bytes accessed | tf_op | source)
XLA Modules:
  0.0 424.4 jit_solution(13714087114713897889)
XLA Ops:
  9.0 2.8 convolution_convert_fusion.1
  11.8 5.2 %copy.17 = bf16[512,4,1024]{2,1,0:T(4,128)(2,1)} copy(bf16[512,4,1024]{2,0,1:T(8,128)(2,1)S(1)} %convolution_convert_fusion.1) | data formatting | bytes 8388608 | tf_op jit(solution)/shard_map/convert_element_type | solution.py:78
  17.0 6.9 %reshape.89 = bf16[256,8,1024]{2,1,0:T(8,128)(2,1)} reshape(bf16[512,4,1024]{2,1,0:T(4,128)(2,1)} %copy.17) | data formatting | bytes 8388608 | tf_op jit(solution)/shard_map/reshape | solution.py:78
  23.9 16.6 %all-to-all-start = ((bf16[256,8,1024]{2,1,0:T(8,128)(2,1)}), bf16[256,8,1024]{2,1,0:T(8,128)(2,1)}, u32[]{:S(2)}, u32[]{:S(2)}) async-start(bf16[256,8,1024]{2,1,0:T(8,128)(2,1)} %reshape.89), calls=%async_computation | async-start | bytes 8388608 | tf_op jit(solution)/shard_map/all_to_all | solution.py:89
  46.2 5.2 %copy.18 = bf16[512,4,1024]{2,1,0:T(4,128)(2,1)} copy(bf16[512,4,1024]{2,0,1:T(8,128)(2,1)S(1)} %convolution_convert_fusion) | data formatting | bytes 8388608 | tf_op jit(solution)/shard_map/convert_element_type | solution.py:78
  51.4 6.9 %reshape.90 = bf16[256,8,1024]{2,1,0:T(8,128)(2,1)} reshape(bf16[512,4,1024]{2,1,0:T(4,128)(2,1)} %copy.18) | data formatting | bytes 8388608 | tf_op jit(solution)/shard_map/reshape | solution.py:78
  58.3 80.3 %all-to-all-done = bf16[256,8,1024]{2,1,0:T(8,128)(2,1)} async-done(((bf16[256,8,1024]{2,1,0:T(8,128)(2,1)}), bf16[256,8,1024]{2,1,0:T(8,128)(2,1)}, u32[]{:S(2)}, u32[]{:S(2)}) %all-to-all-start) | async-done | bytes 4194336 | tf_op jit(solution)/shard_map/all_to_all | solution.py:89
  138.6 17.3 %all-to-all-start.1 = ((bf16[256,8,1024]{2,1,0:T(8,128)(2,1)}), bf16[256,8,1024]{2,1,0:T(8,128)(2,1)}, u32[]{:S(2)}, u32[]{:S(2)}) async-start(bf16[256,8,1024]{2,1,0:T(8,128)(2,1)} %reshape.90), calls=%async_computation.1 | async-start | bytes 8388608 | tf_op jit(solution)/shard_map/all_to_all | solution.py:91
  157.1 10.3 %all-gather.3.cloned.1.call-done = bf16[2048,1024]{1,0:T(8,128)(2,1)} async-done(((bf16[8,1024]{1,0:T(8,128)(2,1)}), bf16[2048,1024]{1,0:T(8,128)(2,1)}) %all-gather.3.cloned.1.call-update) | async-done | bytes 4194320 | tf_op jit(solution)/shard_map/all_gather | solution.py:86
  176.4 2.9 copy.23
  179.3 7.2 %dot_general.32 = bf16[512,4,1024]{2,1,0:T(4,128)(2,1)} reshape(bf16[256,8,1024]{2,1,0:T(8,128)(2,1)} %all-to-all-done) | data formatting | bytes 8388608 | tf_op jit(solution)/shard_map/dot_general | solution.py:25
  186.5 8.2 %fusion.13 = f32[512,4,1024]{2,0,1:T(8,128)S(1)} fusion(bf16[512,4,1024]{2,1,0:T(4,128)(2,1)} %dot_general.32, bf16[1,1024,1024]{2,1,0:T(8,128)(2,1)S(1)} %copy-done), kind=kOutput, calls=%fused_computation.20 | convolution fusion | flops 4294967296 | bytes 14680064 | tf_op jit(solution)/shard_map/dot_general | solution.py:25
  194.7 3.2 copy-done.2
  199.4 3.5 concatenate.40
  203.0 7.3 %fusion.71 = (f32[512,3,1024]{2,0,1:T(8,128)}, bf16[512,3,1024]{2,0,1:T(8,128)(2,1)S(1)}) fusion(f32[512,4,1024]{2,0,1:T(8,128)} %copy-done.2, f32[512,1024]{1,0:T(8,128)S(1)} %get-tuple-element.31), kind=kLoop, calls=%fused_computation.98 | loop fusion | flops 3145728 | bytes 17825792 | tf_op jit(solution)/shard_map/slice | solution.py:29
  214.7 3.5 fusion.30
  218.2 6.7 %pad_maximum_fusion = bf16[256,3,4,1024]{3,2,1,0:T(4,128)(2,1)} fusion(bf16[256,1,4,1024]{3,2,1,0:T(4,128)(2,1)S(1)} %copy-done.4, bf16[256,2,3,1024]{3,2,1,0:T(4,128)(2,1)S(1)} %bitcast.94, bf16[256,2,1,1024]{3,2,1,0:T(2,128)(2,1)S(1)} %copy-done.5), kind=kLoop, calls=%fused_computation | loop fusion | flops 18874368 | bytes 12582912 | tf_op jit(solution)/shard_map/concatenate | solution.py:96
  224.9 28.7 %all-to-all-done.1 = bf16[256,8,1024]{2,1,0:T(8,128)(2,1)} async-done(((bf16[256,8,1024]{2,1,0:T(8,128)(2,1)}), bf16[256,8,1024]{2,1,0:T(8,128)(2,1)}, u32[]{:S(2)}, u32[]{:S(2)}) %all-to-all-start.1) | async-done | bytes 4194336 | tf_op jit(solution)/shard_map/all_to_all | solution.py:91
  253.7 7.3 %all-to-all-start.2 = ((bf16[256,3,4,1024]{3,2,1,0:T(4,128)(2,1)}), bf16[256,3,4,1024]{3,2,1,0:T(4,128)(2,1)}, u32[]{:S(2)}, u32[]{:S(2)}) async-start(bf16[256,3,4,1024]{3,2,1,0:T(4,128)(2,1)} %pad_maximum_fusion), calls=%async_computation.2 | async-start | bytes 12582912 | tf_op jit(solution)/shard_map/all_to_all | solution.py:102
  262.9 2.7 copy_convert_fusion
  265.7 8.8 %reshape.94 = f32[512,4,1024]{2,1,0:T(4,128)} reshape(bf16[256,8,1024]{2,1,0:T(8,128)(2,1)} %all-to-all-done.1) | data formatting | bytes 12582912 | tf_op jit(solution)/shard_map/convert_element_type | solution.py:38
  274.5 8.8 %slice.74 = f32[512,3,1024]{2,1,0:T(4,128)} slice(f32[512,4,1024]{2,1,0:T(4,128)} %reshape.94), slice={[0:512], [1:4], [0:1024]} | slice | bytes 12582912 | tf_op jit(solution)/shard_map/slice | solution.py:39
  283.2 13.1 %multiply_reduce_fusion = (f32[512,1024]{1,0:T(8,128)}, bf16[512,3,1024]{2,0,1:T(8,128)(2,1)}) fusion(f32[512,3,1024]{2,0,1:T(8,128)} %get-tuple-element.17, f32[512,3,1024]{2,1,0:T(4,128)} %slice.74, f32[512,1024]{1,0:T(8,128)} %fusion.30), kind=kLoop, calls=%fused_computation.2 | loop fusion | flops 5767168 | bytes 19922944 | tf_op jit(solution)/shard_map/reduce_sum | solution.py:39
  296.3 3.4 fusion.69
  300.1 5.2 %copy.27 = bf16[512,4,1024]{2,1,0:T(4,128)(2,1)} copy(bf16[512,4,1024]{2,0,1:T(8,128)(2,1)S(1)} %pad_maximum_fusion.1) | data formatting | bytes 8388608 | tf_op jit(solution)/shard_map/concatenate | solution.py:43
  305.3 7.1 %reshape.92 = bf16[2048,1024]{1,0:T(8,128)(2,1)} reshape(bf16[512,4,1024]{2,1,0:T(4,128)(2,1)} %copy.27) | data formatting | bytes 8388608 | tf_op jit(solution)/shard_map/reshape | solution.py:46
  312.4 4.0 multiply_reduce_fusion.1
  318.6 6.5 %fusion.9 = f32[1024,1024]{1,0:T(8,128)S(1)} fusion(bf16[2048,1024]{1,0:T(8,128)(2,1)S(1)} %copy-done.8, bf16[256,8,1024]{2,1,0:T(8,128)(2,1)} %all-to-all-done), kind=kOutput, calls=%fused_computation.16 | convolution fusion | flops 4294967296 | bytes 12582912 | tf_op jit(solution)/shard_map/dot_general | solution.py:44
  325.1 5.1 %fusion.38 = bf16[1,1024,1024]{2,1,0:T(8,128)(2,1)} fusion(f32[1024,1024]{1,0:T(8,128)S(1)} %fusion.9, bf16[256,3,1024]{2,0,1:T(8,128)(2,1)S(1)} %get-tuple-element.43, bf16[256,1,1024]{2,0,1:T(8,128)(2,1)S(1)} %get-tuple-element.37, bf16[256,4,1024]{2,1,0:T(4,128)(2,1)S(1)} %copy-done.10), kind=kOutput, calls=%fused_computation.57 | convolution fusion | flops 2150629376 | bytes 10485760 | tf_op jit(solution)/shard_map/dot_general | solution.py:44
  330.2 72.6 %all-to-all-done.2 = bf16[256,3,4,1024]{3,2,1,0:T(4,128)(2,1)} async-done(((bf16[256,3,4,1024]{3,2,1,0:T(4,128)(2,1)}), bf16[256,3,4,1024]{3,2,1,0:T(4,128)(2,1)}, u32[]{:S(2)}, u32[]{:S(2)}) %all-to-all-start.2) | async-done | bytes 6291488 | tf_op jit(solution)/shard_map/all_to_all | solution.py:102
  405.1 4.3 %slice.70 = bf16[256,2,4,1024]{3,2,1,0:T(4,128)(2,1)S(1)} slice(bf16[256,3,4,1024]{3,2,1,0:T(4,128)(2,1)} %all-to-all-done.2), slice={[0:256], [0:2], [0:4], [0:1024]} | slice | bytes 8388608 | tf_op jit(solution)/shard_map/slice | solution.py:112
  409.4 3.1 select_bitcast_fusion.1
  (60 shorter events, 32.5 us)
Async XLA Ops:
  7.2 163.0 %copy-start = (bf16[1,1024,1024]{2,1,0:T(8,128)(2,1)S(1)}, bf16[1,1024,1024]{2,1,0:T(8,128)(2,1)}, u32[]{:S(2)}) copy-start(bf16[1,1024,1024]{2,1,0:T(8,128)(2,1)} %param.12) | copy-start | bytes 6291460
  23.9 16.7 %copy-start.11 = (bf16[256,1024]{1,0:T(8,128)(2,1)S(1)}, bf16[256,1024]{1,0:T(8,128)(2,1)}, u32[]{:S(2)}) copy-start(bf16[256,1024]{1,0:T(8,128)(2,1)} %param.10) | copy-start | bytes 1572868
  23.9 16.7 %copy-start.12 = (bf16[256,1024]{1,0:T(8,128)(2,1)S(1)}, bf16[256,1024]{1,0:T(8,128)(2,1)}, u32[]{:S(2)}) copy-start(bf16[256,1024]{1,0:T(8,128)(2,1)} %param.14) | copy-start | bytes 1572868
  23.9 114.7 %all-to-all-start = ((bf16[256,8,1024]{2,1,0:T(8,128)(2,1)}), bf16[256,8,1024]{2,1,0:T(8,128)(2,1)}, u32[]{:S(2)}, u32[]{:S(2)}) async-start(bf16[256,8,1024]{2,1,0:T(8,128)(2,1)} %reshape.89), calls=%async_computation | async-start | bytes 8388608 | tf_op jit(solution)/shard_map/all_to_all | solution.py:89
  40.5 126.9 %all-gather.3.cloned.1.call-start = ((), (), s32[]{:S(2)}) async-start(), calls=%async_computation.3 | async-start | bytes 4210688 | tf_op jit(solution)/shard_map/all_gather | solution.py:86
  58.3 97.6 %copy-start.14 = (s32[256]{0:T(256)S(1)}, s32[256]{0:T(256)}, u32[]{:S(2)}) copy-start(s32[256]{0:T(256)} %param.9) | copy-start | bytes 3076
  58.3 98.2 %copy-start.13 = (bf16[1,1024]{1,0:T(2,128)(2,1)S(1)}, bf16[1,1024]{1,0:T(2,128)(2,1)}, u32[]{:S(2)}) copy-start(bf16[1,1024]{1,0:T(2,128)(2,1)} %param.13) | copy-start | bytes 6148
  138.6 115.0 %all-to-all-start.1 = ((bf16[256,8,1024]{2,1,0:T(8,128)(2,1)}), bf16[256,8,1024]{2,1,0:T(8,128)(2,1)}, u32[]{:S(2)}, u32[]{:S(2)}) async-start(bf16[256,8,1024]{2,1,0:T(8,128)(2,1)} %reshape.90), calls=%async_computation.1 | async-start | bytes 8388608 | tf_op jit(solution)/shard_map/all_to_all | solution.py:91
  170.1 2.6 copy-start.9
  172.8 3.4 copy-start.7
  194.7 3.2 copy-start.2
  213.0 5.2 %copy-start.4 = (bf16[256,1,4,1024]{3,2,1,0:T(4,128)(2,1)S(1)}, bf16[256,1,4,1024]{3,2,1,0:T(4,128)(2,1)}, u32[]{:S(2)}) copy-start(bf16[256,1,4,1024]{3,2,1,0:T(4,128)(2,1)} %copy.23) | copy-start | bytes 6291460
  213.0 5.2 %copy-start.5 = (bf16[256,2,1,1024]{3,2,1,0:T(2,128)(2,1)S(1)}, bf16[256,2,1,1024]{3,2,1,0:T(2,128)(2,1)}, u32[]{:S(2)}) copy-start(bf16[256,2,1,1024]{3,2,1,0:T(2,128)(2,1)} %concatenate.40) | copy-start | bytes 3145732
  253.7 9.3 %copy-start.6 = (bf16[256,4,1024]{2,1,0:T(4,128)(2,1)S(1)}, bf16[256,4,1024]{2,1,0:T(4,128)(2,1)}, u32[]{:S(2)}) copy-start(bf16[256,4,1024]{2,1,0:T(4,128)(2,1)} %get-tuple-element.44) | copy-start | bytes 6291460
  253.7 149.1 %all-to-all-start.2 = ((bf16[256,3,4,1024]{3,2,1,0:T(4,128)(2,1)}), bf16[256,3,4,1024]{3,2,1,0:T(4,128)(2,1)}, u32[]{:S(2)}, u32[]{:S(2)}) async-start(bf16[256,3,4,1024]{3,2,1,0:T(4,128)(2,1)} %pad_maximum_fusion), calls=%async_computation.2 | async-start | bytes 12582912 | tf_op jit(solution)/shard_map/all_to_all | solution.py:102
  283.2 13.1 %slice-start = ((f32[512,4,1024]{2,1,0:T(4,128)}), f32[512,1,1024]{2,1,0:T(1,128)S(1)}, s32[]{:S(2)}) async-start(f32[512,4,1024]{2,1,0:T(4,128)} %reshape.94), calls=%async_computation.4 | async-start | bytes 4194304 | tf_op jit(solution)/shard_map/slice | solution.py:39
  296.3 3.4 copy-start.3
  312.4 6.2 %copy-start.8 = (bf16[2048,1024]{1,0:T(8,128)(2,1)S(1)}, bf16[2048,1024]{1,0:T(8,128)(2,1)}, u32[]{:S(2)}) copy-start(bf16[2048,1024]{1,0:T(8,128)(2,1)} %reshape.92) | copy-start | bytes 12582916
  318.6 6.5 %copy-start.10 = (bf16[256,4,1024]{2,1,0:T(4,128)(2,1)S(1)}, bf16[256,4,1024]{2,1,0:T(4,128)(2,1)}, u32[]{:S(2)}) copy-start(bf16[256,4,1024]{2,1,0:T(4,128)(2,1)} %copy-done.9) | copy-start | bytes 6291460
  412.5 4.9 %copy-start.1 = (bf16[1,1024,1024]{2,1,0:T(8,128)(2,1)S(1)}, bf16[1,1024,1024]{2,1,0:T(8,128)(2,1)}, u32[]{:S(2)}) copy-start(bf16[1,1024,1024]{2,1,0:T(8,128)(2,1)} %param.12) | copy-start | bytes 6291460
Sparse Core Ops, SparseCore 0:
  45.6 121.7 all-gather.2
